TPU v7x, 1024 devices: a whole 8x8x8 slice. The times are simulated.
1024 devices in a mesh: ctx: 16 (over z, core), head: 8 (over y), dp: 8 (over x).
Axes of the slice: x: 8, y: 8, z: 8, core: 2. Of those that a mesh axis runs over, the one named last changes fastest.
Arguments:
- queries: bfloat16 [32768, 4096], P(('ctx', 'dp'), 'head'), may hold values from -4 to 4
- key_states: bfloat16 [32768, 1024], P(('ctx', 'dp'), 'head'), may hold values from -4 to 4
- value_states: bfloat16 [32768, 1024], P(('ctx', 'dp'), 'head'), may hold values from -4 to 4
- out_grad: bfloat16 [32768, 4096], P(('ctx', 'dp'), 'head'), may hold values from -24 to 24
- out_proj: bfloat16 [4096, 4096], P('head'), may hold values from -0.09375 to 0.09375
- local_span: int32 [256], P(('ctx', 'dp')), may hold values from 1 to 2
- stride_reach: int32 [256], P(('ctx', 'dp')), may hold values from 0 to 4
Outputs:
- d_queries: bfloat16 [32768, 4096], P(('ctx', 'dp'), 'head')
- d_keys: bfloat16 [32768, 1024], P(('ctx', 'dp'), 'head')
- d_values: bfloat16 [32768, 1024], P(('ctx', 'dp'), 'head')
- d_out_proj: float32 [4096, 4096], P(('head', 'dp'), 'ctx')
All inputs are finite; a program needn't handle non-finite values.
Results may differ from a plain program's by a relative error of at most 0.017.
Values may be sent and summed in bfloat16 or wider, within the bound.
No kernel may reach another device: no remote copies, remote signals or barrier semaphores. Data moves between devices by JAX's collectives and lax.ppermute only.
A program may use at most 64 MiB of HBM per device.

v0:
```python
import math

import jax
import jax.numpy as jnp
from jax import lax
from jax.sharding import PartitionSpec as P

HD = 128
BLK = 128
REACH = 4


def passed_along(x, axis, by):
    peers = lax.axis_size(axis)
    pairs = [(i, i + by) for i in range(peers) if 0 <= i + by < peers]
    return lax.ppermute(x, axis, pairs)


def pair_masks(span_table, reaches, device, seq_rows, block, reach_count):
    stride = seq_rows // block
    positions = jnp.arange(seq_rows, dtype=jnp.int32)
    row_block = positions // block
    block_ids = jnp.arange(stride, dtype=jnp.int32)
    picked = row_block[:, None] == block_ids[None, :]
    span_row = jnp.sum(jnp.where(picked, span_table[None, :], 0), axis=1, dtype=jnp.int32)
    reach_row = jnp.sum(jnp.where(picked, reaches[None, :], 0), axis=1, dtype=jnp.int32)
    own_mask = (positions[None, :] <= positions[:, None]) & (
        row_block[None, :] >= row_block[:, None] - span_row[:, None] + 1
    )
    distances = jnp.arange(1, reach_count + 1, dtype=jnp.int32)
    query_block = device * stride + row_block
    far_block = device * stride - 1 - (distances - 1) * stride
    far_mask = (device >= distances)[None, :] & (
        (distances[None, :] <= reach_row[:, None])
        | (far_block[None, :] >= query_block[:, None] - span_row[:, None] + 1)
    )
    return jnp.concatenate([own_mask, jnp.repeat(far_mask, block, axis=1)], axis=1)


def attend_both(query_rows, key_rows, value_rows, grad_attended, allowed, kv_count, head_size):
    seq_rows = query_rows.shape[0]
    group_size = query_rows.shape[1] // (kv_count * head_size)
    scaling = 1.0 / math.sqrt(head_size)
    query_heads = query_rows.reshape(seq_rows, kv_count, group_size, head_size)
    key_heads = key_rows.reshape(-1, kv_count, head_size)
    value_heads = value_rows.reshape(-1, kv_count, head_size)
    grad_heads = grad_attended.reshape(seq_rows, kv_count, group_size, head_size)
    scores = (
        jnp.einsum("skgd,tkd->kgst", query_heads, key_heads, preferred_element_type=jnp.float32)
        * scaling
    )
    raised = jnp.where(allowed, jnp.exp(scores), 0.0)
    weights = raised / jnp.sum(raised, axis=-1, keepdims=True)
    rounded_weights = weights.astype(jnp.bfloat16)
    attended = jnp.einsum(
        "kgst,tkd->skgd", rounded_weights, value_heads, preferred_element_type=jnp.float32
    )
    attended = attended.astype(jnp.bfloat16).reshape(seq_rows, -1)
    d_weights = jnp.einsum(
        "skgd,tkd->kgst", grad_heads, value_heads, preferred_element_type=jnp.float32
    )
    row_dot = jnp.sum(weights * d_weights, axis=-1, keepdims=True)
    d_scores = (weights * (d_weights - row_dot) * scaling).astype(jnp.bfloat16)
    d_query = jnp.einsum("kgst,tkd->skgd", d_scores, key_heads, preferred_element_type=jnp.float32)
    d_query = d_query.astype(jnp.bfloat16).reshape(seq_rows, -1)
    d_key_all = jnp.einsum(
        "kgst,skgd->tkd", d_scores, query_heads, preferred_element_type=jnp.float32
    ).reshape(-1, kv_count * head_size)
    d_value_all = jnp.einsum(
        "kgst,skgd->tkd", rounded_weights, grad_heads, preferred_element_type=jnp.float32
    ).reshape(-1, kv_count * head_size)
    return (attended, d_query, d_key_all, d_value_all)


def local(queries, key_states, value_states, out_grad, out_proj, local_span, stride_reach):
    seq_rows = key_states.shape[0]
    kv_width = key_states.shape[1]
    kv_count = kv_width // HD
    device = lax.axis_index(("ctx", "dp"))
    summary_keys = key_states[seq_rows - BLK :]
    summary_values = value_states[seq_rows - BLK :]
    far_key_list = []
    far_value_list = []
    for distance in range(1, REACH + 1):
        moved_keys, moved_values = passed_along(
            (summary_keys, summary_values), ("ctx", "dp"), distance
        )
        far_key_list.append(moved_keys)
        far_value_list.append(moved_values)
    all_keys = jnp.concatenate([key_states] + far_key_list, axis=0)
    all_values = jnp.concatenate([value_states] + far_value_list, axis=0)
    grad_rows = lax.all_gather(out_grad, "head", axis=1, tiled=True)
    grad_attended = lax.dot_general(
        grad_rows, out_proj, (((1,), (1,)), ((), ())), preferred_element_type=jnp.float32
    ).astype(jnp.bfloat16)
    allowed = pair_masks(local_span, stride_reach, device, seq_rows, BLK, REACH)
    attended, d_query, d_key_all, d_value_all = attend_both(
        queries, all_keys, all_values, grad_attended, allowed, kv_count, HD
    )
    returned_keys = jnp.zeros((BLK, kv_width), jnp.float32)
    returned_values = jnp.zeros((BLK, kv_width), jnp.float32)
    for distance in range(1, REACH + 1):
        lower = seq_rows + (distance - 1) * BLK
        back_keys, back_values = passed_along(
            (d_key_all[lower : lower + BLK], d_value_all[lower : lower + BLK]),
            ("ctx", "dp"),
            -distance,
        )
        returned_keys = returned_keys + back_keys
        returned_values = returned_values + back_values
    d_keys = jnp.concatenate(
        [d_key_all[: seq_rows - BLK], d_key_all[seq_rows - BLK : seq_rows] + returned_keys], axis=0
    ).astype(jnp.bfloat16)
    d_values = jnp.concatenate(
        [d_value_all[: seq_rows - BLK], d_value_all[seq_rows - BLK : seq_rows] + returned_values],
        axis=0,
    ).astype(jnp.bfloat16)
    partial_cols = lax.psum_scatter(
        lax.dot_general(
            grad_rows, attended, (((0,), (0,)), ((), ())), preferred_element_type=jnp.float32
        ).astype(jnp.bfloat16),
        "ctx",
        scatter_dimension=0,
        tiled=True,
    ).astype(jnp.float32)
    d_out_proj = lax.psum_scatter(partial_cols, "dp", scatter_dimension=1, tiled=True).T
    return (d_query, d_keys, d_values, d_out_proj)


def solution(mesh):
    in_specs = (
        P(("ctx", "dp"), "head"),
        P(("ctx", "dp"), "head"),
        P(("ctx", "dp"), "head"),
        P(("ctx", "dp"), "head"),
        P("head", None),
        P(("ctx", "dp")),
        P(("ctx", "dp")),
    )
    out_specs = (
        P(("ctx", "dp"), "head"),
        P(("ctx", "dp"), "head"),
        P(("ctx", "dp"), "head"),
        P(("head", "dp"), "ctx"),
    )
    return jax.shard_map(local, mesh=mesh, in_specs=in_specs, out_specs=out_specs, check_vma=False)
```

profile of v0, /device:TPU:14, one launch (start us, length us, event | category | flops | bytes accessed | tf_op | source)
XLA Modules:
  0.0 193.6 jit_solution(15378186085393410410)
XLA Ops:
  8.7 1.9 collective-permute-start
  10.6 3.8 %collective-permute-start.1 = (bf16[128,128]{1,0:T(8,128)(2,1)S(1)}, bf16[128,128]{1,0:T(8,128)(2,1)S(1)}, u32[]{:S(2)}, u32[]{:S(2)}) collective-permute-start(bf16[128,128]{1,0:T(8,128)(2,1)S(1)} %slice.80), channel_id=1, source_target_pairs={{0,2},{1,3},{2,4},{3,5},{4,6},{5,7},{6,64},{7,65},{64,66},{65,67},... | collective-permute-start | bytes 98312 | tf_op jit(solution)/shard_map/ppermute | solution.py:16
  14.5 5.3 %collective-permute-start.2 = (bf16[128,128]{1,0:T(8,128)(2,1)S(1)}, bf16[128,128]{1,0:T(8,128)(2,1)S(1)}, u32[]{:S(2)}, u32[]{:S(2)}) collective-permute-start(bf16[128,128]{1,0:T(8,128)(2,1)S(1)} %slice.80), channel_id=1, source_target_pairs={{0,3},{1,4},{2,5},{3,6},{4,7},{5,64},{6,65},{7,66},{64,67},{65,68}... | collective-permute-start | bytes 98312 | tf_op jit(solution)/shard_map/ppermute | solution.py:16
  19.8 6.5 %collective-permute-start.3 = (bf16[128,128]{1,0:T(8,128)(2,1)S(1)}, bf16[128,128]{1,0:T(8,128)(2,1)S(1)}, u32[]{:S(2)}, u32[]{:S(2)}) collective-permute-start(bf16[128,128]{1,0:T(8,128)(2,1)S(1)} %slice.80), channel_id=1, source_target_pairs={{0,4},{1,5},{2,6},{3,7},{4,64},{5,65},{6,66},{7,67},{64,68},{65,69... | collective-permute-start | bytes 98312 | tf_op jit(solution)/shard_map/ppermute | solution.py:16
  27.1 3.1 %collective-permute-start.4 = (bf16[128,128]{1,0:T(8,128)(2,1)S(1)}, bf16[128,128]{1,0:T(8,128)(2,1)S(1)}, u32[]{:S(2)}, u32[]{:S(2)}) collective-permute-start(bf16[128,128]{1,0:T(8,128)(2,1)S(1)} %slice.81), channel_id=1, source_target_pairs={{0,1},{1,2},{2,3},{3,4},{4,5},{5,6},{6,7},{7,64},{64,65},{65,66},{... | collective-permute-start | bytes 98312 | tf_op jit(solution)/shard_map/ppermute | solution.py:16
  33.1 5.5 %collective-permute-start.5 = (bf16[128,128]{1,0:T(8,128)(2,1)S(1)}, bf16[128,128]{1,0:T(8,128)(2,1)S(1)}, u32[]{:S(2)}, u32[]{:S(2)}) collective-permute-start(bf16[128,128]{1,0:T(8,128)(2,1)S(1)} %slice.81), channel_id=1, source_target_pairs={{0,2},{1,3},{2,4},{3,5},{4,6},{5,7},{6,64},{7,65},{64,66},{65,67},... | collective-permute-start | bytes 98312 | tf_op jit(solution)/shard_map/ppermute | solution.py:16
  38.6 2.6 %collective-permute-start.6 = (bf16[128,128]{1,0:T(8,128)(2,1)S(1)}, bf16[128,128]{1,0:T(8,128)(2,1)S(1)}, u32[]{:S(2)}, u32[]{:S(2)}) collective-permute-start(bf16[128,128]{1,0:T(8,128)(2,1)S(1)} %slice.81), channel_id=1, source_target_pairs={{0,3},{1,4},{2,5},{3,6},{4,7},{5,64},{6,65},{7,66},{64,67},{65,68}... | collective-permute-start | bytes 98312 | tf_op jit(solution)/shard_map/ppermute | solution.py:16
  41.2 4.2 %collective-permute-start.7 = (bf16[128,128]{1,0:T(8,128)(2,1)S(1)}, bf16[128,128]{1,0:T(8,128)(2,1)S(1)}, u32[]{:S(2)}, u32[]{:S(2)}) collective-permute-start(bf16[128,128]{1,0:T(8,128)(2,1)S(1)} %slice.81), channel_id=1, source_target_pairs={{0,4},{1,5},{2,6},{3,7},{4,64},{5,65},{6,66},{7,67},{64,68},{65,69... | collective-permute-start | bytes 98312 | tf_op jit(solution)/shard_map/ppermute | solution.py:16
  46.7 4.3 %collective-permute-done.7 = bf16[128,128]{1,0:T(8,128)(2,1)S(1)} collective-permute-done((bf16[128,128]{1,0:T(8,128)(2,1)S(1)}, bf16[128,128]{1,0:T(8,128)(2,1)S(1)}, u32[]{:S(2)}, u32[]{:S(2)}) %collective-permute-start.7) | collective-permute-done | bytes 32800 | tf_op jit(solution)/shard_map/ppermute | solution.py:16
  53.5 14.7 %all-gather.2.cloned.1.call-done = bf16[256,4096]{1,0:T(8,128)(2,1)} async-done(((bf16[256,512]{1,0:T(8,128)(2,1)}), bf16[256,4096]{1,0:T(8,128)(2,1)}) %all-gather.2.cloned.1.call-update) | async-done | bytes 2097168 | tf_op jit(solution)/shard_map/all_gather | solution.py:92
  68.2 4.9 %fusion = bf16[4096,512]{0,1:T(8,128)(2,1)} fusion(bf16[256,512]{0,1:T(8,128)(2,1)} %bitcast.146, bf16[256,4096]{1,0:T(8,128)(2,1)} %all-gather.2.cloned.1.call-done), kind=kOutput, calls=%fused_computation.1 | convolution fusion | flops 1075838976 | bytes 6553600 | tf_op jit(solution)/shard_map/dot_general | solution.py:119
  73.2 4.8 %convolution_convert_fusion.2 = bf16[256,512]{1,0:T(8,128)(2,1)} fusion(bf16[256,4096]{1,0:T(8,128)(2,1)} %all-gather.2.cloned.1.call-done, bf16[512,4096]{1,0:T(8,128)(2,1)} %param.11), kind=kOutput, calls=%fused_computation.21 | convolution fusion | flops 1073872896 | bytes 6553600 | tf_op jit(solution)/shard_map/dot_general | solution.py:93
  79.8 2.0 %fusion.13 = f32[768,1,128]{0,2,1:T(8,128)S(1)} fusion(bf16[256,4,128]{0,2,1:T(8,128)(2,1)} %bitcast.147, f32[4,256]{1,0:T(4,128)S(1)} %get-tuple-element.24, f32[768,256,4]{1,0,2:T(8,128)S(1)} %get-tuple-element.25, pred[256,768]{0,1:T(8,128)(4,1)} %copy-done.1), kind=kOutput, calls=%fused_computation.17 | convolution fusion | flops 204472320 | bytes 4001792 | tf_op jit(solution)/shard_map/kgst,skgd->tkd/dot_general | solution.py:69
  82.6 3.3 %collective-permute-start.12 = (f32[128,128]{0,1:T(8,128)}, f32[128,128]{0,1:T(8,128)S(1)}, u32[]{:S(2)}, u32[]{:S(2)}) collective-permute-start(f32[128,128]{0,1:T(8,128)} %get-tuple-element.17), channel_id=1, source_target_pairs={{1,0},{2,1},{3,2},{4,3},{5,4},{6,5},{7,6},{64,7},{65,64},{66,65},{... | collective-permute-start | bytes 196616 | tf_op jit(solution)/shard_map/ppermute | solution.py:16
  85.9 4.5 %collective-permute-start.13 = (f32[128,128]{0,1:T(8,128)}, f32[128,128]{0,1:T(8,128)S(1)}, u32[]{:S(2)}, u32[]{:S(2)}) collective-permute-start(f32[128,128]{0,1:T(8,128)} %get-tuple-element.14), channel_id=1, source_target_pairs={{2,0},{3,1},{4,2},{5,3},{6,4},{7,5},{64,6},{65,7},{66,64},{67,65},... | collective-permute-start | bytes 196616 | tf_op jit(solution)/shard_map/ppermute | solution.py:16
  90.5 2.2 %collective-permute-start.14 = (f32[128,128]{0,1:T(8,128)}, f32[128,128]{0,1:T(8,128)}, u32[]{:S(2)}, u32[]{:S(2)}) collective-permute-start(f32[128,128]{0,1:T(8,128)} %get-tuple-element.16), channel_id=1, source_target_pairs={{3,0},{4,1},{5,2},{6,3},{7,4},{64,5},{65,6},{66,7},{67,64},{68,65}... | collective-permute-start | bytes 196616 | tf_op jit(solution)/shard_map/ppermute | solution.py:16
  92.7 1.9 collective-permute-start.15
  97.7 45.7 %reduce-scatter.3.cloned.1.call-done = bf16[256,512]{0,1:T(8,128)(2,1)} async-done(((bf16[4096,512]{0,1:T(8,128)(2,1)}), bf16[256,512]{0,1:T(8,128)(2,1)}) %reduce-scatter.3.cloned.1.call-update) | async-done | bytes 262160 | tf_op jit(solution)/shard_map/reduce_scatter | solution.py:118
  146.0 5.0 %collective-permute-start.10 = (f32[128,128]{1,0:T(8,128)S(1)}, f32[128,128]{1,0:T(8,128)S(1)}, u32[]{:S(2)}, u32[]{:S(2)}) collective-permute-start(f32[128,128]{1,0:T(8,128)S(1)} %get-tuple-element.20), channel_id=1, source_target_pairs={{3,0},{4,1},{5,2},{6,3},{7,4},{64,5},{65,6},{66,7},{67,64},{68,65}... | collective-permute-start | bytes 196616 | tf_op jit(solution)/shard_map/ppermute | solution.py:16
  151.9 2.4 %collective-permute-start.11 = (f32[128,128]{1,0:T(8,128)S(1)}, f32[128,128]{1,0:T(8,128)S(1)}, u32[]{:S(2)}, u32[]{:S(2)}) collective-permute-start(f32[128,128]{1,0:T(8,128)S(1)} %get-tuple-element.19), channel_id=1, source_target_pairs={{4,0},{5,1},{6,2},{7,3},{64,4},{65,5},{66,6},{67,7},{68,64},{69,65... | collective-permute-start | bytes 196616 | tf_op jit(solution)/shard_map/ppermute | solution.py:16
  154.3 1.9 collective-permute-start.8
  156.3 2.6 %collective-permute-start.9 = (f32[128,128]{1,0:T(8,128)S(1)}, f32[128,128]{1,0:T(8,128)S(1)}, u32[]{:S(2)}, u32[]{:S(2)}) collective-permute-start(f32[128,128]{1,0:T(8,128)S(1)} %get-tuple-element.18), channel_id=1, source_target_pairs={{2,0},{3,1},{4,2},{5,3},{6,4},{7,5},{64,6},{65,7},{66,64},{67,65},... | collective-permute-start | bytes 196616 | tf_op jit(solution)/shard_map/ppermute | solution.py:16
  161.8 2.6 %collective-permute-done.9 = f32[128,128]{1,0:T(8,128)S(1)} collective-permute-done((f32[128,128]{1,0:T(8,128)S(1)}, f32[128,128]{1,0:T(8,128)S(1)}, u32[]{:S(2)}, u32[]{:S(2)}) %collective-permute-start.9) | collective-permute-done | bytes 65568 | tf_op jit(solution)/shard_map/ppermute | solution.py:16
  165.1 22.0 %reduce-scatter.5.cloned.1.call-done = f32[256,64]{0,1:T(8,128)} async-done(((f32[256,512]{0,1:T(8,128)}), f32[256,64]{0,1:T(8,128)}) %reduce-scatter.5.cloned.1.call-update) | async-done | bytes 65552 | tf_op jit(solution)/shard_map/reduce_scatter | solution.py:126
  (77 shorter events, 21.4 us)
Async XLA Ops:
  7.2 43.8 %copy-start = (bf16[256,512]{1,0:T(8,128)(2,1)S(1)}, bf16[256,512]{1,0:T(8,128)(2,1)}, u32[]{:S(2)}) copy-start(bf16[256,512]{1,0:T(8,128)(2,1)} %param.7) | copy-start | bytes 786436
  7.2 61.0 %all-gather.2.cloned.1.call-start = ((), (), s32[]{:S(2)}) async-start(), calls=%async_computation.2 | async-start | bytes 2359296 | tf_op jit(solution)/shard_map/all_gather | solution.py:92
  7.9 135.5 %reduce-scatter.3.cloned.1.call-start = ((), (), s32[]{:S(2)}) async-start(), calls=%async_computation.3 | async-start | bytes 4456448 | tf_op jit(solution)/shard_map/reduce_scatter | solution.py:118
  8.7 24.3 %collective-permute-start = (bf16[128,128]{1,0:T(8,128)(2,1)S(1)}, bf16[128,128]{1,0:T(8,128)(2,1)S(1)}, u32[]{:S(2)}, u32[]{:S(2)}) collective-permute-start(bf16[128,128]{1,0:T(8,128)(2,1)S(1)} %slice.80), channel_id=1, source_target_pairs={{0,1},{1,2},{2,3},{3,4},{4,5},{5,6},{6,7},{7,64},{64,65},{65,66},{... | collective-permute-start | bytes 98312 | tf_op jit(solution)/shard_map/ppermute | solution.py:16
  10.6 28.0 %collective-permute-start.1 = (bf16[128,128]{1,0:T(8,128)(2,1)S(1)}, bf16[128,128]{1,0:T(8,128)(2,1)S(1)}, u32[]{:S(2)}, u32[]{:S(2)}) collective-permute-start(bf16[128,128]{1,0:T(8,128)(2,1)S(1)} %slice.80), channel_id=1, source_target_pairs={{0,2},{1,3},{2,4},{3,5},{4,6},{5,7},{6,64},{7,65},{64,66},{65,67},... | collective-permute-start | bytes 98312 | tf_op jit(solution)/shard_map/ppermute | solution.py:16
  14.5 26.7 %collective-permute-start.2 = (bf16[128,128]{1,0:T(8,128)(2,1)S(1)}, bf16[128,128]{1,0:T(8,128)(2,1)S(1)}, u32[]{:S(2)}, u32[]{:S(2)}) collective-permute-start(bf16[128,128]{1,0:T(8,128)(2,1)S(1)} %slice.80), channel_id=1, source_target_pairs={{0,3},{1,4},{2,5},{3,6},{4,7},{5,64},{6,65},{7,66},{64,67},{65,68}... | collective-permute-start | bytes 98312 | tf_op jit(solution)/shard_map/ppermute | solution.py:16
  19.8 25.7 %collective-permute-start.3 = (bf16[128,128]{1,0:T(8,128)(2,1)S(1)}, bf16[128,128]{1,0:T(8,128)(2,1)S(1)}, u32[]{:S(2)}, u32[]{:S(2)}) collective-permute-start(bf16[128,128]{1,0:T(8,128)(2,1)S(1)} %slice.80), channel_id=1, source_target_pairs={{0,4},{1,5},{2,6},{3,7},{4,64},{5,65},{6,66},{7,67},{64,68},{65,69... | collective-permute-start | bytes 98312 | tf_op jit(solution)/shard_map/ppermute | solution.py:16
  27.1 18.4 %collective-permute-start.4 = (bf16[128,128]{1,0:T(8,128)(2,1)S(1)}, bf16[128,128]{1,0:T(8,128)(2,1)S(1)}, u32[]{:S(2)}, u32[]{:S(2)}) collective-permute-start(bf16[128,128]{1,0:T(8,128)(2,1)S(1)} %slice.81), channel_id=1, source_target_pairs={{0,1},{1,2},{2,3},{3,4},{4,5},{5,6},{6,7},{7,64},{64,65},{65,66},{... | collective-permute-start | bytes 98312 | tf_op jit(solution)/shard_map/ppermute | solution.py:16
  32.1 19.7 %copy-start.1 = (pred[256,768]{0,1:T(8,128)(4,1)}, pred[256,768]{0,1:T(8,128)(4,1)S(1)}, u32[]{:S(2)}) copy-start(pred[256,768]{0,1:T(8,128)(4,1)S(1)} %pad_add_fusion) | copy-start | bytes 589828
  33.1 12.5 %collective-permute-start.5 = (bf16[128,128]{1,0:T(8,128)(2,1)S(1)}, bf16[128,128]{1,0:T(8,128)(2,1)S(1)}, u32[]{:S(2)}, u32[]{:S(2)}) collective-permute-start(bf16[128,128]{1,0:T(8,128)(2,1)S(1)} %slice.81), channel_id=1, source_target_pairs={{0,2},{1,3},{2,4},{3,5},{4,6},{5,7},{6,64},{7,65},{64,66},{65,67},... | collective-permute-start | bytes 98312 | tf_op jit(solution)/shard_map/ppermute | solution.py:16
  38.6 8.0 %collective-permute-start.6 = (bf16[128,128]{1,0:T(8,128)(2,1)S(1)}, bf16[128,128]{1,0:T(8,128)(2,1)S(1)}, u32[]{:S(2)}, u32[]{:S(2)}) collective-permute-start(bf16[128,128]{1,0:T(8,128)(2,1)S(1)} %slice.81), channel_id=1, source_target_pairs={{0,3},{1,4},{2,5},{3,6},{4,7},{5,64},{6,65},{7,66},{64,67},{65,68}... | collective-permute-start | bytes 98312 | tf_op jit(solution)/shard_map/ppermute | solution.py:16
  41.2 9.7 %collective-permute-start.7 = (bf16[128,128]{1,0:T(8,128)(2,1)S(1)}, bf16[128,128]{1,0:T(8,128)(2,1)S(1)}, u32[]{:S(2)}, u32[]{:S(2)}) collective-permute-start(bf16[128,128]{1,0:T(8,128)(2,1)S(1)} %slice.81), channel_id=1, source_target_pairs={{0,4},{1,5},{2,6},{3,7},{4,64},{5,65},{6,66},{7,67},{64,68},{65,69... | collective-permute-start | bytes 98312 | tf_op jit(solution)/shard_map/ppermute | solution.py:16
  73.1 113.9 %reduce-scatter.5.cloned.1.call-start = ((), (), s32[]{:S(2)}) async-start(), calls=%async_computation.4 | async-start | bytes 589824 | tf_op jit(solution)/shard_map/reduce_scatter | solution.py:126
  79.8 14.8 %copy-start.2 = (pred[256,768]{0,1:T(8,128)(4,1)S(1)}, pred[256,768]{0,1:T(8,128)(4,1)}, u32[]{:S(2)}) copy-start(pred[256,768]{0,1:T(8,128)(4,1)} %copy-done.1) | copy-start | bytes 589828
  79.8 14.9 %copy-start.6 = (bf16[256,512]{0,1:T(8,128)(2,1)S(1)}, bf16[256,512]{0,1:T(8,128)(2,1)}, u32[]{:S(2)}) copy-start(bf16[256,512]{0,1:T(8,128)(2,1)} %copy.40) | copy-start | bytes 786436
  79.8 14.9 %copy-start.8 = (bf16[768,128]{1,0:T(8,128)(2,1)S(1)}, bf16[768,128]{1,0:T(8,128)(2,1)}, u32[]{:S(2)}) copy-start(bf16[768,128]{1,0:T(8,128)(2,1)} %copy-done.7) | copy-start | bytes 589828
  82.6 69.3 %collective-permute-start.12 = (f32[128,128]{0,1:T(8,128)}, f32[128,128]{0,1:T(8,128)S(1)}, u32[]{:S(2)}, u32[]{:S(2)}) collective-permute-start(f32[128,128]{0,1:T(8,128)} %get-tuple-element.17), channel_id=1, source_target_pairs={{1,0},{2,1},{3,2},{4,3},{5,4},{6,5},{7,6},{64,7},{65,64},{66,65},{... | collective-permute-start | bytes 196616 | tf_op jit(solution)/shard_map/ppermute | solution.py:16
  85.9 68.4 %collective-permute-start.13 = (f32[128,128]{0,1:T(8,128)}, f32[128,128]{0,1:T(8,128)S(1)}, u32[]{:S(2)}, u32[]{:S(2)}) collective-permute-start(f32[128,128]{0,1:T(8,128)} %get-tuple-element.14), channel_id=1, source_target_pairs={{2,0},{3,1},{4,2},{5,3},{6,4},{7,5},{64,6},{65,7},{66,64},{67,65},... | collective-permute-start | bytes 196616 | tf_op jit(solution)/shard_map/ppermute | solution.py:16
  90.5 65.8 %collective-permute-start.14 = (f32[128,128]{0,1:T(8,128)}, f32[128,128]{0,1:T(8,128)}, u32[]{:S(2)}, u32[]{:S(2)}) collective-permute-start(f32[128,128]{0,1:T(8,128)} %get-tuple-element.16), channel_id=1, source_target_pairs={{3,0},{4,1},{5,2},{6,3},{7,4},{64,5},{65,6},{66,7},{67,64},{68,65}... | collective-permute-start | bytes 196616 | tf_op jit(solution)/shard_map/ppermute | solution.py:16
  92.7 66.2 %collective-permute-start.15 = (f32[128,128]{0,1:T(8,128)}, f32[128,128]{0,1:T(8,128)}, u32[]{:S(2)}, u32[]{:S(2)}) collective-permute-start(f32[128,128]{0,1:T(8,128)} %get-tuple-element.15), channel_id=1, source_target_pairs={{4,0},{5,1},{6,2},{7,3},{64,4},{65,5},{66,6},{67,7},{68,64},{69,65... | collective-permute-start | bytes 196616 | tf_op jit(solution)/shard_map/ppermute | solution.py:16
  146.0 14.6 %collective-permute-start.10 = (f32[128,128]{1,0:T(8,128)S(1)}, f32[128,128]{1,0:T(8,128)S(1)}, u32[]{:S(2)}, u32[]{:S(2)}) collective-permute-start(f32[128,128]{1,0:T(8,128)S(1)} %get-tuple-element.20), channel_id=1, source_target_pairs={{3,0},{4,1},{5,2},{6,3},{7,4},{64,5},{65,6},{66,7},{67,64},{68,65}... | collective-permute-start | bytes 196616 | tf_op jit(solution)/shard_map/ppermute | solution.py:16
  151.9 9.6 %collective-permute-start.11 = (f32[128,128]{1,0:T(8,128)S(1)}, f32[128,128]{1,0:T(8,128)S(1)}, u32[]{:S(2)}, u32[]{:S(2)}) collective-permute-start(f32[128,128]{1,0:T(8,128)S(1)} %get-tuple-element.19), channel_id=1, source_target_pairs={{4,0},{5,1},{6,2},{7,3},{64,4},{65,5},{66,6},{67,7},{68,64},{69,65... | collective-permute-start | bytes 196616 | tf_op jit(solution)/shard_map/ppermute | solution.py:16
  154.3 7.5 %collective-permute-start.8 = (f32[128,128]{1,0:T(8,128)S(1)}, f32[128,128]{1,0:T(8,128)S(1)}, u32[]{:S(2)}, u32[]{:S(2)}) collective-permute-start(f32[128,128]{1,0:T(8,128)S(1)} %get-tuple-element.21), channel_id=1, source_target_pairs={{1,0},{2,1},{3,2},{4,3},{5,4},{6,5},{7,6},{64,7},{65,64},{66,65},{... | collective-permute-start | bytes 196616 | tf_op jit(solution)/shard_map/ppermute | solution.py:16
  156.3 8.2 %collective-permute-start.9 = (f32[128,128]{1,0:T(8,128)S(1)}, f32[128,128]{1,0:T(8,128)S(1)}, u32[]{:S(2)}, u32[]{:S(2)}) collective-permute-start(f32[128,128]{1,0:T(8,128)S(1)} %get-tuple-element.18), channel_id=1, source_target_pairs={{2,0},{3,1},{4,2},{5,3},{6,4},{7,5},{64,6},{65,7},{66,64},{67,65},... | collective-permute-start | bytes 196616 | tf_op jit(solution)/shard_map/ppermute | solution.py:16
  (4 other events, 21.7 us)
Sparse Core Ops, SparseCore 0:
  10.7 57.4 all-gather.1
  73.2 70.0 reduce-scatter.2
  147.3 39.6 reduce-scatter.4
where the time goes:
time: 195 us; the launch traced here: 194 us
  waiting for transfers between devices  92.4 us (47%)
  starting transfers between devices  57 us (29%)
  matrix products  16.1 us (8%)
  between operations  14.2 us (7%)
  local copies, waits for them, and re-layouts  8.47 us (4%)
  other arithmetic  5.34 us (3%)
    ppermute x16, starting transfers between devices, passed_along(): return lax.ppermute(x, axis, pairs)  56.9 us
    reduce_scatter x1, waiting for transfers between devices, local(): lax.psum_scatter(lax.dot_general(grad_rows, attended, (((0,), (0,)), ((),...  45.7 us
    reduce_scatter x1, waiting for transfers between devices, local(): lax.psum_scatter(partial_cols, 'dp', scatter_dimension=1, tiled=True)  22 us
    all_gather x1, waiting for transfers between devices, local(): grad_rows = lax.all_gather(out_grad, 'head', axis=1, tiled=True)  14.7 us
    ppermute x16, waiting for transfers between devices, passed_along(): return lax.ppermute(x, axis, pairs)  9.26 us
    dot_general x1, matrix products, local(): lax.dot_general(grad_rows, attended, (((0,), (0,)), ((), ())), preferred_...  4.88 us
    dot_general x1, matrix products, local(): lax.dot_general(grad_rows, out_proj, (((1,), (1,)), ((), ())), preferred_...  4.81 us
  transfers between devices with their start and end apart: 19, of which 8 were waited for; matrix products, arithmetic and copies ran while one was open for 13% of the time, Pallas kernels for 0%

commit v1 on v0

--- a/solution.py
+++ b/solution.py
@@ -16,6 +16,22 @@
     return lax.ppermute(x, axis, pairs)
 
 
+def exchange_sum(x, axis):
+    peers = lax.axis_size(axis)
+    me = lax.axis_index(axis)
+    levels = peers.bit_length() - 1
+    rest = x.shape[1:]
+    total = x.reshape((2,) * levels + (x.shape[0] // peers,) + rest)
+    total = total.transpose(tuple(reversed(range(levels))) + tuple(range(levels, total.ndim)))
+    total = total.reshape(x.shape)
+    for level in range(levels):
+        span = 1 << level
+        half = total.shape[0] // 2
+        upper = (me // span) % 2 == 1
+        keep = jnp.where(upper, total[half:], total[:half])
+        give = jnp.where(upper, total[:half], total[half:])
+        total = keep + lax.ppermute(give, axis, [(i, i ^ span) for i in range(peers)])
+    return total
 def pair_masks(span_table, reaches, device, seq_rows, block, reach_count):
     stride = seq_rows // block
     positions = jnp.arange(seq_rows, dtype=jnp.int32)
@@ -77,16 +93,15 @@
     kv_width = key_states.shape[1]
     kv_count = kv_width // HD
     device = lax.axis_index(("ctx", "dp"))
-    summary_keys = key_states[seq_rows - BLK :]
-    summary_values = value_states[seq_rows - BLK :]
+    summary = jnp.concatenate(
+        [key_states[seq_rows - BLK :], value_states[seq_rows - BLK :]], axis=1
+    )
     far_key_list = []
     far_value_list = []
     for distance in range(1, REACH + 1):
-        moved_keys, moved_values = passed_along(
-            (summary_keys, summary_values), ("ctx", "dp"), distance
-        )
-        far_key_list.append(moved_keys)
-        far_value_list.append(moved_values)
+        moved = passed_along(summary, ("ctx", "dp"), distance)
+        far_key_list.append(moved[:, :kv_width])
+        far_value_list.append(moved[:, kv_width:])
     all_keys = jnp.concatenate([key_states] + far_key_list, axis=0)
     all_values = jnp.concatenate([value_states] + far_value_list, axis=0)
     grad_rows = lax.all_gather(out_grad, "head", axis=1, tiled=True)
@@ -101,13 +116,15 @@
     returned_values = jnp.zeros((BLK, kv_width), jnp.float32)
     for distance in range(1, REACH + 1):
         lower = seq_rows + (distance - 1) * BLK
-        back_keys, back_values = passed_along(
-            (d_key_all[lower : lower + BLK], d_value_all[lower : lower + BLK]),
+        back = passed_along(
+            jnp.concatenate(
+                [d_key_all[lower : lower + BLK], d_value_all[lower : lower + BLK]], axis=1
+            ),
             ("ctx", "dp"),
             -distance,
         )
-        returned_keys = returned_keys + back_keys
-        returned_values = returned_values + back_values
+        returned_keys = returned_keys + back[:, :kv_width]
+        returned_values = returned_values + back[:, kv_width:]
     d_keys = jnp.concatenate(
         [d_key_all[: seq_rows - BLK], d_key_all[seq_rows - BLK : seq_rows] + returned_keys], axis=0
     ).astype(jnp.bfloat16)
@@ -123,7 +140,7 @@
         scatter_dimension=0,
         tiled=True,
     ).astype(jnp.float32)
-    d_out_proj = lax.psum_scatter(partial_cols, "dp", scatter_dimension=1, tiled=True).T
+    d_out_proj = exchange_sum(partial_cols.T, "dp")
     return (d_query, d_keys, d_values, d_out_proj)
 
 

time: 195 us -> 185 us (0.949)
  starting transfers between devices: 57 us -> 42.5 us
  waiting for transfers between devices: 92.4 us -> 97.3 us
    ppermute x16 -> x8, starting transfers between devices: 56.9 us -> 32 us  [passed_along(): return lax.ppermute(x, axis, pairs)]
    reduce_scatter x1 -> x0, waiting for transfers between devices: 22 us -> none  [local(): lax.psum_scatter(partial_cols, 'dp', scatter_dimension=1, tiled=True)]
    all_gather x1, waiting for transfers between devices: 14.7 us -> 33.9 us  [local(): grad_rows = lax.all_gather(out_grad, 'head', axis=1, tiled=True)]
    ppermute x0 -> x3, waiting for transfers between devices: none -> 13.6 us  [exchange_sum(): lax.ppermute(give, axis, [(i, i ^ span) for i in range(peers)])]
    ppermute x0 -> x3, starting transfers between devices: none -> 10.4 us  [exchange_sum(): lax.ppermute(give, axis, [(i, i ^ span) for i in range(peers)])]
    ppermute x16 -> x8, waiting for transfers between devices: 9.26 us -> 0.83 us  [passed_along(): return lax.ppermute(x, axis, pairs)]
    reduce_scatter x1, waiting for transfers between devices: 45.7 us -> 48.3 us  [local(): lax.psum_scatter(lax.dot_general(grad_rows, attended, (((0,), (0,)), ((),...]
    unnamed x28 -> x23, local copies, waits for them, and re-layouts: 3.45 us -> 4 us
  transfers between devices with their start and end apart: 19 -> 13, of which waited for: 8 -> 6; matrix products, arithmetic and copies ran while one was open for 13% -> 13% of each run, Pallas kernels for 0% -> 0%
where the time goes in v1:
time: 185 us; the launch traced here: 184 us
  waiting for transfers between devices  97.3 us (53%)
  starting transfers between devices  42.5 us (23%)
  matrix products  16.2 us (9%)
  between operations  14.6 us (8%)
  local copies, waits for them, and re-layouts  8.55 us (5%)
  other arithmetic  4.68 us (3%)
    reduce_scatter x1, waiting for transfers between devices, local(): lax.psum_scatter(lax.dot_general(grad_rows, attended, (((0,), (0,)), ((),...  48.3 us
    all_gather x1, waiting for transfers between devices, local(): grad_rows = lax.all_gather(out_grad, 'head', axis=1, tiled=True)  33.9 us
    ppermute x8, starting transfers between devices, passed_along(): return lax.ppermute(x, axis, pairs)  32 us
    ppermute x3, waiting for transfers between devices, exchange_sum(): lax.ppermute(give, axis, [(i, i ^ span) for i in range(peers)])  13.6 us
    ppermute x3, starting transfers between devices, exchange_sum(): lax.ppermute(give, axis, [(i, i ^ span) for i in range(peers)])  10.4 us
    dot_general x1, matrix products, local(): lax.dot_general(grad_rows, attended, (((0,), (0,)), ((), ())), preferred_...  4.9 us
    dot_general x1, matrix products, local(): lax.dot_general(grad_rows, out_proj, (((1,), (1,)), ((), ())), preferred_...  4.82 us
    unnamed x23, local copies, waits for them, and re-layouts  4 us
  transfers between devices with their start and end apart: 13, of which 6 were waited for; matrix products, arithmetic and copies ran while one was open for 13% of the time, Pallas kernels for 0%

profile of v1, /device:TPU:14, one launch (start us, length us, event | category | flops | bytes accessed | tf_op | source)
XLA Modules:
  0.0 183.8 jit_solution(13823105645902204933)
XLA Ops:
  9.5 1.9 %collective-permute-start = (bf16[128,256]{1,0:T(8,128)(2,1)S(1)}, bf16[128,256]{1,0:T(8,128)(2,1)S(1)}, u32[]{:S(2)}, u32[]{:S(2)}) collective-permute-start(bf16[128,256]{1,0:T(8,128)(2,1)S(1)} %pad_maximum_fusion.4), channel_id=1, source_target_pairs={{0,1},{1,2},{2,3},{3,4},{4,5},{5,6},{6,7},{7,64},{64,65},{65,66},{... | collective-permute-start | bytes 196616 | tf_op jit(solution)/shard_map/ppermute | solution.py:16
  11.4 3.8 %collective-permute-start.1 = (bf16[128,256]{1,0:T(8,128)(2,1)S(1)}, bf16[128,256]{1,0:T(8,128)(2,1)S(1)}, u32[]{:S(2)}, u32[]{:S(2)}) collective-permute-start(bf16[128,256]{1,0:T(8,128)(2,1)S(1)} %pad_maximum_fusion.4), channel_id=1, source_target_pairs={{0,2},{1,3},{2,4},{3,5},{4,6},{5,7},{6,64},{7,65},{64,66},{65,67},... | collective-permute-start | bytes 196616 | tf_op jit(solution)/shard_map/ppermute | solution.py:16
  15.3 5.3 %collective-permute-start.2 = (bf16[128,256]{1,0:T(8,128)(2,1)S(1)}, bf16[128,256]{1,0:T(8,128)(2,1)S(1)}, u32[]{:S(2)}, u32[]{:S(2)}) collective-permute-start(bf16[128,256]{1,0:T(8,128)(2,1)S(1)} %pad_maximum_fusion.4), channel_id=1, source_target_pairs={{0,3},{1,4},{2,5},{3,6},{4,7},{5,64},{6,65},{7,66},{64,67},{65,68}... | collective-permute-start | bytes 196616 | tf_op jit(solution)/shard_map/ppermute | solution.py:16
  20.5 6.5 %collective-permute-start.3 = (bf16[128,256]{1,0:T(8,128)(2,1)S(1)}, bf16[128,256]{1,0:T(8,128)(2,1)S(1)}, u32[]{:S(2)}, u32[]{:S(2)}) collective-permute-start(bf16[128,256]{1,0:T(8,128)(2,1)S(1)} %pad_maximum_fusion.4), channel_id=1, source_target_pairs={{0,4},{1,5},{2,6},{3,7},{4,64},{5,65},{6,66},{7,67},{64,68},{65,69... | collective-permute-start | bytes 196616 | tf_op jit(solution)/shard_map/ppermute | solution.py:16
  27.1 1.1 copy.49
  32.7 1.6 fusion.16
  34.3 33.9 %all-gather.2.cloned.1.call-done = bf16[256,4096]{1,0:T(8,128)(2,1)} async-done(((bf16[256,512]{1,0:T(8,128)(2,1)}), bf16[256,4096]{1,0:T(8,128)(2,1)}) %all-gather.2.cloned.1.call-update) | async-done | bytes 2097168 | tf_op jit(solution)/shard_map/all_gather | solution.py:107
  68.2 4.9 %fusion = bf16[4096,512]{0,1:T(8,128)(2,1)} fusion(bf16[256,512]{0,1:T(8,128)(2,1)} %bitcast.141, bf16[256,4096]{1,0:T(8,128)(2,1)} %all-gather.2.cloned.1.call-done), kind=kOutput, calls=%fused_computation.1 | convolution fusion | flops 1075838976 | bytes 6553600 | tf_op jit(solution)/shard_map/dot_general | solution.py:136
  73.2 4.8 %convolution_convert_fusion.2 = bf16[256,512]{1,0:T(8,128)(2,1)} fusion(bf16[256,4096]{1,0:T(8,128)(2,1)} %all-gather.2.cloned.1.call-done, bf16[512,4096]{1,0:T(8,128)(2,1)} %param.11), kind=kOutput, calls=%fused_computation.21 | convolution fusion | flops 1073872896 | bytes 6553600 | tf_op jit(solution)/shard_map/dot_general | solution.py:108
  78.0 1.8 copy.50
  79.8 2.0 %fusion.13 = f32[768,1,128]{0,2,1:T(8,128)S(1)} fusion(bf16[256,4,128]{0,2,1:T(8,128)(2,1)} %bitcast.143, f32[4,256]{1,0:T(4,128)S(1)} %get-tuple-element.36, f32[768,256,4]{1,0,2:T(8,128)S(1)} %get-tuple-element.37, pred[256,768]{0,1:T(8,128)(4,1)} %copy-done), kind=kOutput, calls=%fused_computation.17 | convolution fusion | flops 204472320 | bytes 4001792 | tf_op jit(solution)/shard_map/kgst,skgd->tkd/dot_general | solution.py:85
  81.9 1.0 fusion.1
  84.6 3.4 %collective-permute-start.4 = (f32[128,256]{0,1:T(8,128)S(1)}, f32[128,256]{0,1:T(8,128)S(1)}, u32[]{:S(2)}, u32[]{:S(2)}) collective-permute-start(f32[128,256]{0,1:T(8,128)S(1)} %pad_maximum_fusion), channel_id=1, source_target_pairs={{1,0},{2,1},{3,2},{4,3},{5,4},{6,5},{7,6},{64,7},{65,64},{66,65},{... | collective-permute-start | bytes 393224 | tf_op jit(solution)/shard_map/ppermute | solution.py:16
  88.0 4.3 %collective-permute-start.5 = (f32[128,256]{0,1:T(8,128)S(1)}, f32[128,256]{0,1:T(8,128)S(1)}, u32[]{:S(2)}, u32[]{:S(2)}) collective-permute-start(f32[128,256]{0,1:T(8,128)S(1)} %pad_maximum_fusion.1), channel_id=1, source_target_pairs={{2,0},{3,1},{4,2},{5,3},{6,4},{7,5},{64,6},{65,7},{66,64},{67,65},... | collective-permute-start | bytes 393224 | tf_op jit(solution)/shard_map/ppermute | solution.py:16
  92.2 2.5 %collective-permute-start.6 = (f32[128,256]{0,1:T(8,128)S(1)}, f32[128,256]{0,1:T(8,128)S(1)}, u32[]{:S(2)}, u32[]{:S(2)}) collective-permute-start(f32[128,256]{0,1:T(8,128)S(1)} %pad_maximum_fusion.2), channel_id=1, source_target_pairs={{3,0},{4,1},{5,2},{6,3},{7,4},{64,5},{65,6},{66,7},{67,64},{68,65}... | collective-permute-start | bytes 393224 | tf_op jit(solution)/shard_map/ppermute | solution.py:16
  95.2 48.3 %reduce-scatter.2.cloned.1.call-done = bf16[256,512]{0,1:T(8,128)(2,1)} async-done(((bf16[4096,512]{0,1:T(8,128)(2,1)}), bf16[256,512]{0,1:T(8,128)(2,1)}) %reduce-scatter.2.cloned.1.call-update) | async-done | bytes 262160 | tf_op jit(solution)/shard_map/reduce_scatter | solution.py:135
  143.4 1.0 transpose.73
  144.5 3.1 %collective-permute-start.8 = (f32[256,256]{1,0:T(8,128)S(1)}, f32[256,256]{1,0:T(8,128)S(1)}, u32[]{:S(2)}, u32[]{:S(2)}) collective-permute-start(f32[256,256]{1,0:T(8,128)S(1)} %bitcast.142), channel_id=1, source_target_pairs={{0,1},{1,0},{2,3},{3,2},{4,5},{5,4},{6,7},{7,6},{8,9},{9,8},{10,11... | collective-permute-start | bytes 786440 | tf_op jit(solution)/shard_map/ppermute | solution.py:33
  147.7 4.3 %collective-permute-start.7 = (f32[128,256]{0,1:T(8,128)S(1)}, f32[128,256]{0,1:T(8,128)S(1)}, u32[]{:S(2)}, u32[]{:S(2)}) collective-permute-start(f32[128,256]{0,1:T(8,128)S(1)} %pad_maximum_fusion.3), channel_id=1, source_target_pairs={{4,0},{5,1},{6,2},{7,3},{64,4},{65,5},{66,6},{67,7},{68,64},{69,65... | collective-permute-start | bytes 393224 | tf_op jit(solution)/shard_map/ppermute | solution.py:16
  152.9 4.4 %collective-permute-done.8 = f32[256,256]{1,0:T(8,128)S(1)} collective-permute-done((f32[256,256]{1,0:T(8,128)S(1)}, f32[256,256]{1,0:T(8,128)S(1)}, u32[]{:S(2)}, u32[]{:S(2)}) %collective-permute-start.8) | collective-permute-done | bytes 262176 | tf_op jit(solution)/shard_map/ppermute | solution.py:33
  157.4 1.9 %collective-permute-start.9 = (f32[128,256]{1,0:T(8,128)S(1)}, f32[128,256]{1,0:T(8,128)S(1)}, u32[]{:S(2)}, u32[]{:S(2)}) collective-permute-start(f32[128,256]{1,0:T(8,128)S(1)} %slice_select_fusion.2), channel_id=1, source_target_pairs={{0,2},{1,3},{2,0},{3,1},{4,6},{5,7},{6,4},{7,5},{8,10},{9,11},{10,... | collective-permute-start | bytes 393224 | tf_op jit(solution)/shard_map/ppermute | solution.py:33
  161.0 4.6 %collective-permute-done.9 = f32[128,256]{1,0:T(8,128)S(1)} collective-permute-done((f32[128,256]{1,0:T(8,128)S(1)}, f32[128,256]{1,0:T(8,128)S(1)}, u32[]{:S(2)}, u32[]{:S(2)}) %collective-permute-start.9) | collective-permute-done | bytes 131104 | tf_op jit(solution)/shard_map/ppermute | solution.py:33
  165.6 5.4 %collective-permute-start.10 = (f32[64,256]{1,0:T(8,128)S(1)}, f32[64,256]{1,0:T(8,128)S(1)}, u32[]{:S(2)}, u32[]{:S(2)}) collective-permute-start(f32[64,256]{1,0:T(8,128)S(1)} %slice_select_fusion.3), channel_id=1, source_target_pairs={{0,4},{1,5},{2,6},{3,7},{4,0},{5,1},{6,2},{7,3},{8,12},{9,13},{10,... | collective-permute-start | bytes 196616 | tf_op jit(solution)/shard_map/ppermute | solution.py:33
  171.7 4.6 %collective-permute-done.10 = f32[64,256]{1,0:T(8,128)S(1)} collective-permute-done((f32[64,256]{1,0:T(8,128)S(1)}, f32[64,256]{1,0:T(8,128)S(1)}, u32[]{:S(2)}, u32[]{:S(2)}) %collective-permute-start.10) | collective-permute-done | bytes 65568 | tf_op jit(solution)/shard_map/ppermute | solution.py:33
  (71 shorter events, 12.8 us)
Async XLA Ops:
  7.2 61.0 %all-gather.2.cloned.1.call-start = ((), (), s32[]{:S(2)}) async-start(), calls=%async_computation.1 | async-start | bytes 2359296 | tf_op jit(solution)/shard_map/all_gather | solution.py:107
  7.9 135.6 %reduce-scatter.2.cloned.1.call-start = ((), (), s32[]{:S(2)}) async-start(), calls=%async_computation.2 | async-start | bytes 4456448 | tf_op jit(solution)/shard_map/reduce_scatter | solution.py:135
  9.5 20.8 %collective-permute-start = (bf16[128,256]{1,0:T(8,128)(2,1)S(1)}, bf16[128,256]{1,0:T(8,128)(2,1)S(1)}, u32[]{:S(2)}, u32[]{:S(2)}) collective-permute-start(bf16[128,256]{1,0:T(8,128)(2,1)S(1)} %pad_maximum_fusion.4), channel_id=1, source_target_pairs={{0,1},{1,2},{2,3},{3,4},{4,5},{5,6},{6,7},{7,64},{64,65},{65,66},{... | collective-permute-start | bytes 196616 | tf_op jit(solution)/shard_map/ppermute | solution.py:16
  11.4 18.9 %collective-permute-start.1 = (bf16[128,256]{1,0:T(8,128)(2,1)S(1)}, bf16[128,256]{1,0:T(8,128)(2,1)S(1)}, u32[]{:S(2)}, u32[]{:S(2)}) collective-permute-start(bf16[128,256]{1,0:T(8,128)(2,1)S(1)} %pad_maximum_fusion.4), channel_id=1, source_target_pairs={{0,2},{1,3},{2,4},{3,5},{4,6},{5,7},{6,64},{7,65},{64,66},{65,67},... | collective-permute-start | bytes 196616 | tf_op jit(solution)/shard_map/ppermute | solution.py:16
  15.3 15.0 %collective-permute-start.2 = (bf16[128,256]{1,0:T(8,128)(2,1)S(1)}, bf16[128,256]{1,0:T(8,128)(2,1)S(1)}, u32[]{:S(2)}, u32[]{:S(2)}) collective-permute-start(bf16[128,256]{1,0:T(8,128)(2,1)S(1)} %pad_maximum_fusion.4), channel_id=1, source_target_pairs={{0,3},{1,4},{2,5},{3,6},{4,7},{5,64},{6,65},{7,66},{64,67},{65,68}... | collective-permute-start | bytes 196616 | tf_op jit(solution)/shard_map/ppermute | solution.py:16
  20.5 10.6 %collective-permute-start.3 = (bf16[128,256]{1,0:T(8,128)(2,1)S(1)}, bf16[128,256]{1,0:T(8,128)(2,1)S(1)}, u32[]{:S(2)}, u32[]{:S(2)}) collective-permute-start(bf16[128,256]{1,0:T(8,128)(2,1)S(1)} %pad_maximum_fusion.4), channel_id=1, source_target_pairs={{0,4},{1,5},{2,6},{3,7},{4,64},{5,65},{6,66},{7,67},{64,68},{65,69... | collective-permute-start | bytes 196616 | tf_op jit(solution)/shard_map/ppermute | solution.py:16
  29.3 3.4 %copy-start = (pred[256,768]{0,1:T(8,128)(4,1)}, pred[256,768]{0,1:T(8,128)(4,1)S(1)}, u32[]{:S(2)}) copy-start(pred[256,768]{0,1:T(8,128)(4,1)S(1)} %pad_add_fusion) | copy-start | bytes 589828
  31.1 0.7 copy-start.2
  31.2 1.5 copy-start.6
  79.8 2.1 %copy-start.1 = (pred[256,768]{0,1:T(8,128)(4,1)S(1)}, pred[256,768]{0,1:T(8,128)(4,1)}, u32[]{:S(2)}) copy-start(pred[256,768]{0,1:T(8,128)(4,1)} %copy-done) | copy-start | bytes 589828
  79.8 2.1 %copy-start.5 = (bf16[256,512]{0,1:T(8,128)(2,1)S(1)}, bf16[256,512]{0,1:T(8,128)(2,1)}, u32[]{:S(2)}) copy-start(bf16[256,512]{0,1:T(8,128)(2,1)} %copy.50) | copy-start | bytes 786436
  79.8 2.1 %copy-start.7 = (bf16[768,128]{1,0:T(8,128)(2,1)S(1)}, bf16[768,128]{1,0:T(8,128)(2,1)}, u32[]{:S(2)}) copy-start(bf16[768,128]{1,0:T(8,128)(2,1)} %copy-done.6) | copy-start | bytes 589828
  81.8 12.9 %copy-start.4 = (f32[768,1,128]{0,2,1:T(8,128)}, f32[768,1,128]{0,2,1:T(8,128)S(1)}, u32[]{:S(2)}) copy-start(f32[768,1,128]{0,2,1:T(8,128)S(1)} %fusion.13) | copy-start | bytes 1179652
  83.9 10.9 %copy-start.3 = (bf16[768,128]{1,0:T(8,128)(2,1)S(1)}, bf16[768,128]{1,0:T(8,128)(2,1)}, u32[]{:S(2)}) copy-start(bf16[768,128]{1,0:T(8,128)(2,1)} %copy-done.2) | copy-start | bytes 589828
  84.6 74.7 %collective-permute-start.4 = (f32[128,256]{0,1:T(8,128)S(1)}, f32[128,256]{0,1:T(8,128)S(1)}, u32[]{:S(2)}, u32[]{:S(2)}) collective-permute-start(f32[128,256]{0,1:T(8,128)S(1)} %pad_maximum_fusion), channel_id=1, source_target_pairs={{1,0},{2,1},{3,2},{4,3},{5,4},{6,5},{7,6},{64,7},{65,64},{66,65},{... | collective-permute-start | bytes 393224 | tf_op jit(solution)/shard_map/ppermute | solution.py:16
  88.0 71.3 %collective-permute-start.5 = (f32[128,256]{0,1:T(8,128)S(1)}, f32[128,256]{0,1:T(8,128)S(1)}, u32[]{:S(2)}, u32[]{:S(2)}) collective-permute-start(f32[128,256]{0,1:T(8,128)S(1)} %pad_maximum_fusion.1), channel_id=1, source_target_pairs={{2,0},{3,1},{4,2},{5,3},{6,4},{7,5},{64,6},{65,7},{66,64},{67,65},... | collective-permute-start | bytes 393224 | tf_op jit(solution)/shard_map/ppermute | solution.py:16
  92.2 67.1 %collective-permute-start.6 = (f32[128,256]{0,1:T(8,128)S(1)}, f32[128,256]{0,1:T(8,128)S(1)}, u32[]{:S(2)}, u32[]{:S(2)}) collective-permute-start(f32[128,256]{0,1:T(8,128)S(1)} %pad_maximum_fusion.2), channel_id=1, source_target_pairs={{3,0},{4,1},{5,2},{6,3},{7,4},{64,5},{65,6},{66,7},{67,64},{68,65}... | collective-permute-start | bytes 393224 | tf_op jit(solution)/shard_map/ppermute | solution.py:16
  144.5 12.8 %collective-permute-start.8 = (f32[256,256]{1,0:T(8,128)S(1)}, f32[256,256]{1,0:T(8,128)S(1)}, u32[]{:S(2)}, u32[]{:S(2)}) collective-permute-start(f32[256,256]{1,0:T(8,128)S(1)} %bitcast.142), channel_id=1, source_target_pairs={{0,1},{1,0},{2,3},{3,2},{4,5},{5,4},{6,7},{7,6},{8,9},{9,8},{10,11... | collective-permute-start | bytes 786440 | tf_op jit(solution)/shard_map/ppermute | solution.py:33
  147.7 11.6 %collective-permute-start.7 = (f32[128,256]{0,1:T(8,128)S(1)}, f32[128,256]{0,1:T(8,128)S(1)}, u32[]{:S(2)}, u32[]{:S(2)}) collective-permute-start(f32[128,256]{0,1:T(8,128)S(1)} %pad_maximum_fusion.3), channel_id=1, source_target_pairs={{4,0},{5,1},{6,2},{7,3},{64,4},{65,5},{66,6},{67,7},{68,64},{69,65... | collective-permute-start | bytes 393224 | tf_op jit(solution)/shard_map/ppermute | solution.py:16
  157.4 8.2 %collective-permute-start.9 = (f32[128,256]{1,0:T(8,128)S(1)}, f32[128,256]{1,0:T(8,128)S(1)}, u32[]{:S(2)}, u32[]{:S(2)}) collective-permute-start(f32[128,256]{1,0:T(8,128)S(1)} %slice_select_fusion.2), channel_id=1, source_target_pairs={{0,2},{1,3},{2,0},{3,1},{4,6},{5,7},{6,4},{7,5},{8,10},{9,11},{10,... | collective-permute-start | bytes 393224 | tf_op jit(solution)/shard_map/ppermute | solution.py:33
  165.6 10.8 %collective-permute-start.10 = (f32[64,256]{1,0:T(8,128)S(1)}, f32[64,256]{1,0:T(8,128)S(1)}, u32[]{:S(2)}, u32[]{:S(2)}) collective-permute-start(f32[64,256]{1,0:T(8,128)S(1)} %slice_select_fusion.3), channel_id=1, source_target_pairs={{0,4},{1,5},{2,6},{3,7},{4,0},{5,1},{6,2},{7,3},{8,12},{9,13},{10,... | collective-permute-start | bytes 196616 | tf_op jit(solution)/shard_map/ppermute | solution.py:33
Sparse Core Ops, SparseCore 0:
  10.7 57.4 all-gather.1
  73.2 70.1 reduce-scatter.1

commit v2 on v1

--- a/solution.py
+++ b/solution.py
@@ -8,6 +8,7 @@
 HD = 128
 BLK = 128
 REACH = 4
+CTX = ("z", "core")
 
 
 def passed_along(x, axis, by):
@@ -92,14 +93,14 @@
     seq_rows = key_states.shape[0]
     kv_width = key_states.shape[1]
     kv_count = kv_width // HD
-    device = lax.axis_index(("ctx", "dp"))
+    device = lax.axis_index(CTX + ("dp",))
     summary = jnp.concatenate(
         [key_states[seq_rows - BLK :], value_states[seq_rows - BLK :]], axis=1
     )
     far_key_list = []
     far_value_list = []
     for distance in range(1, REACH + 1):
-        moved = passed_along(summary, ("ctx", "dp"), distance)
+        moved = passed_along(summary, CTX + ("dp",), distance)
         far_key_list.append(moved[:, :kv_width])
         far_value_list.append(moved[:, kv_width:])
     all_keys = jnp.concatenate([key_states] + far_key_list, axis=0)
@@ -120,7 +121,7 @@
             jnp.concatenate(
                 [d_key_all[lower : lower + BLK], d_value_all[lower : lower + BLK]], axis=1
             ),
-            ("ctx", "dp"),
+            CTX + ("dp",),
             -distance,
         )
         returned_keys = returned_keys + back[:, :kv_width]
@@ -132,32 +133,39 @@
         [d_value_all[: seq_rows - BLK], d_value_all[seq_rows - BLK : seq_rows] + returned_values],
         axis=0,
     ).astype(jnp.bfloat16)
-    partial_cols = lax.psum_scatter(
-        lax.dot_general(
-            grad_rows, attended, (((0,), (0,)), ((), ())), preferred_element_type=jnp.float32
-        ).astype(jnp.bfloat16),
-        "ctx",
-        scatter_dimension=0,
-        tiled=True,
-    ).astype(jnp.float32)
+    term = lax.dot_general(
+        grad_rows, attended, (((0,), (0,)), ((), ())), preferred_element_type=jnp.float32
+    ).astype(jnp.bfloat16)
+    chip_cols = lax.psum_scatter(term, "z", scatter_dimension=0, tiled=True).astype(jnp.float32)
+    half = chip_cols.shape[0] // 2
+    upper = lax.axis_index("core") == 1
+    kept = jnp.where(upper, chip_cols[half:], chip_cols[:half])
+    given = jnp.where(upper, chip_cols[:half], chip_cols[half:])
+    partial_cols = kept + lax.ppermute(given, "core", [(0, 1), (1, 0)])
     d_out_proj = exchange_sum(partial_cols.T, "dp")
     return (d_query, d_keys, d_values, d_out_proj)
 
 
 def solution(mesh):
+    devices = mesh.devices
+    split = jax.sharding.Mesh(
+        devices.reshape(devices.shape[0] // 2, 2, *devices.shape[1:]),
+        CTX + mesh.axis_names[1:],
+    )
+    rows = CTX + ("dp",)
     in_specs = (
-        P(("ctx", "dp"), "head"),
-        P(("ctx", "dp"), "head"),
-        P(("ctx", "dp"), "head"),
-        P(("ctx", "dp"), "head"),
+        P(rows, "head"),
+        P(rows, "head"),
+        P(rows, "head"),
+        P(rows, "head"),
         P("head", None),
-        P(("ctx", "dp")),
-        P(("ctx", "dp")),
+        P(rows),
+        P(rows),
     )
     out_specs = (
-        P(("ctx", "dp"), "head"),
-        P(("ctx", "dp"), "head"),
-        P(("ctx", "dp"), "head"),
-        P(("head", "dp"), "ctx"),
+        P(rows, "head"),
+        P(rows, "head"),
+        P(rows, "head"),
+        P(("head", "dp"), CTX),
     )
-    return jax.shard_map(local, mesh=mesh, in_specs=in_specs, out_specs=out_specs, check_vma=False)
+    return jax.shard_map(local, mesh=split, in_specs=in_specs, out_specs=out_specs, check_vma=False)

time: 185 us -> 191 us (1.032)
  the two profiles are of different devices: /device:TPU:14 before, /device:TPU:1 now
where the time goes in v2:
time: 191 us; the launch traced here: 190 us
  waiting for transfers between devices  85.9 us (45%)
  starting transfers between devices  56.5 us (30%)
  matrix products  16.3 us (9%)
  between operations  14.6 us (8%)
  local copies, waits for them, and re-layouts  9.43 us (5%)
  other arithmetic  6.94 us (4%)
    ppermute x8, starting transfers between devices, passed_along(): return lax.ppermute(x, axis, pairs)  43.2 us
    reduce_scatter x1, waiting for transfers between devices, local(): lax.psum_scatter(term, 'z', scatter_dimension=0, tiled=True)  39.9 us
    all_gather x1, waiting for transfers between devices, local(): grad_rows = lax.all_gather(out_grad, 'head', axis=1, tiled=True)  29.7 us
    ppermute x3, waiting for transfers between devices, exchange_sum(): lax.ppermute(give, axis, [(i, i ^ span) for i in range(peers)])  15.6 us
    ppermute x3, starting transfers between devices, exchange_sum(): lax.ppermute(give, axis, [(i, i ^ span) for i in range(peers)])  10.7 us
    dot_general x1, matrix products, local(): lax.dot_general(grad_rows, attended, (((0,), (0,)), ((), ())), preferred_...  4.89 us
    dot_general x1, matrix products, local(): lax.dot_general(grad_rows, out_proj, (((1,), (1,)), ((), ())), preferred_...  4.81 us
    unnamed x25, local copies, waits for them, and re-layouts  4.02 us
  transfers between devices with their start and end apart: 14, of which 5 were waited for; matrix products, arithmetic and copies ran while one was open for 14% of the time, Pallas kernels for 0%

profile of v2, /device:TPU:1, one launch (start us, length us, event | category | flops | bytes accessed | tf_op | source)
XLA Modules:
  0.0 189.7 jit_solution(16497619809743504786)
XLA Ops:
  9.5 3.9 %collective-permute-start = (bf16[128,256]{1,0:T(8,128)(2,1)S(1)}, bf16[128,256]{1,0:T(8,128)(2,1)S(1)}, u32[]{:S(2)}, u32[]{:S(2)}) collective-permute-start(bf16[128,256]{1,0:T(8,128)(2,1)S(1)} %pad_maximum_fusion.4), channel_id=1, source_target_pairs={{0,1},{1,2},{2,3},{3,4},{4,5},{5,6},{6,7},{7,64},{64,65},{65,66},{... | collective-permute-start | bytes 196616 | tf_op jit(solution)/shard_map/ppermute | solution.py:17
  13.4 4.0 %collective-permute-start.1 = (bf16[128,256]{1,0:T(8,128)(2,1)S(1)}, bf16[128,256]{1,0:T(8,128)(2,1)S(1)}, u32[]{:S(2)}, u32[]{:S(2)}) collective-permute-start(bf16[128,256]{1,0:T(8,128)(2,1)S(1)} %pad_maximum_fusion.4), channel_id=1, source_target_pairs={{0,2},{1,3},{2,4},{3,5},{4,6},{5,7},{6,64},{7,65},{64,66},{65,67},... | collective-permute-start | bytes 196616 | tf_op jit(solution)/shard_map/ppermute | solution.py:17
  17.5 4.4 %collective-permute-start.2 = (bf16[128,256]{1,0:T(8,128)(2,1)S(1)}, bf16[128,256]{1,0:T(8,128)(2,1)S(1)}, u32[]{:S(2)}, u32[]{:S(2)}) collective-permute-start(bf16[128,256]{1,0:T(8,128)(2,1)S(1)} %pad_maximum_fusion.4), channel_id=1, source_target_pairs={{0,3},{1,4},{2,5},{3,6},{4,7},{5,64},{6,65},{7,66},{64,67},{65,68}... | collective-permute-start | bytes 196616 | tf_op jit(solution)/shard_map/ppermute | solution.py:17
  21.9 7.4 %collective-permute-start.3 = (bf16[128,256]{1,0:T(8,128)(2,1)S(1)}, bf16[128,256]{1,0:T(8,128)(2,1)S(1)}, u32[]{:S(2)}, u32[]{:S(2)}) collective-permute-start(bf16[128,256]{1,0:T(8,128)(2,1)S(1)} %pad_maximum_fusion.4), channel_id=1, source_target_pairs={{0,4},{1,5},{2,6},{3,7},{4,64},{5,65},{6,66},{7,67},{64,68},{65,69... | collective-permute-start | bytes 196616 | tf_op jit(solution)/shard_map/ppermute | solution.py:17
  34.1 1.7 fusion.16
  35.8 29.7 %all-gather.2.cloned.1.call-done = bf16[256,4096]{1,0:T(8,128)(2,1)} async-done(((bf16[256,512]{1,0:T(8,128)(2,1)}), bf16[256,4096]{1,0:T(8,128)(2,1)}) %all-gather.2.cloned.1.call-update) | async-done | bytes 2097168 | tf_op jit(solution)/shard_map/all_gather | solution.py:108
  65.5 4.9 %fusion = bf16[4096,512]{0,1:T(8,128)(2,1)} fusion(bf16[256,512]{0,1:T(8,128)(2,1)} %bitcast.141, bf16[256,4096]{1,0:T(8,128)(2,1)} %all-gather.2.cloned.1.call-done), kind=kOutput, calls=%fused_computation.1 | convolution fusion | flops 1075838976 | bytes 6553600 | tf_op jit(solution)/shard_map/dot_general | solution.py:136
  70.5 4.8 %convolution_convert_fusion.2 = bf16[256,512]{1,0:T(8,128)(2,1)} fusion(bf16[256,4096]{1,0:T(8,128)(2,1)} %all-gather.2.cloned.1.call-done, bf16[512,4096]{1,0:T(8,128)(2,1)} %param.11), kind=kOutput, calls=%fused_computation.21 | convolution fusion | flops 1073872896 | bytes 6553600 | tf_op jit(solution)/shard_map/dot_general | solution.py:109
  75.3 1.8 copy.50
  77.1 2.0 %fusion.13 = f32[768,1,128]{0,2,1:T(8,128)S(1)} fusion(bf16[256,4,128]{0,2,1:T(8,128)(2,1)} %bitcast.143, f32[4,256]{1,0:T(4,128)S(1)} %get-tuple-element.36, f32[768,256,4]{1,0,2:T(8,128)S(1)} %get-tuple-element.37, pred[256,768]{0,1:T(8,128)(4,1)} %copy-done.1), kind=kOutput, calls=%fused_computation.17 | convolution fusion | flops 204472320 | bytes 4001792 | tf_op jit(solution)/shard_map/kgst,skgd->tkd/dot_general | solution.py:86
  80.2 2.8 %fusion.7 = bf16[4,256,768]{1,2,0:T(8,128)(2,1)S(1)} fusion(f32[768,256,4]{1,0,2:T(8,128)S(1)} %get-tuple-element.39, f32[4,256]{1,0:T(4,128)S(1)} %get-tuple-element.38, f32[4,256]{1,0:T(4,128)S(1)} %get-tuple-element.36, f32[768,256,4]{1,0,2:T(8,128)} %copy-done, pred[256,768]{0,1:T(8,128)(4,1)S(1)} %copy-done.2), kind=kLoop, calls=%fused_computation.11 | loop fusion | flops 5505024 | bytes 8069120 | tf_op jit(solution)/shard_map/reshape.9
  83.8 8.6 %collective-permute-start.4 = (f32[128,256]{0,1:T(8,128)S(1)}, f32[128,256]{0,1:T(8,128)S(1)}, u32[]{:S(2)}, u32[]{:S(2)}) collective-permute-start(f32[128,256]{0,1:T(8,128)S(1)} %pad_maximum_fusion), channel_id=1, source_target_pairs={{1,0},{2,1},{3,2},{4,3},{5,4},{6,5},{7,6},{64,7},{65,64},{66,65},{... | collective-permute-start | bytes 393224 | tf_op jit(solution)/shard_map/ppermute | solution.py:17
  92.4 4.3 %collective-permute-start.5 = (f32[128,256]{0,1:T(8,128)S(1)}, f32[128,256]{0,1:T(8,128)S(1)}, u32[]{:S(2)}, u32[]{:S(2)}) collective-permute-start(f32[128,256]{0,1:T(8,128)S(1)} %pad_maximum_fusion.1), channel_id=1, source_target_pairs={{2,0},{3,1},{4,2},{5,3},{6,4},{7,5},{64,6},{65,7},{66,64},{67,65},... | collective-permute-start | bytes 393224 | tf_op jit(solution)/shard_map/ppermute | solution.py:17
  96.6 39.9 %reduce-scatter.2.cloned.1.call-done = bf16[512,512]{0,1:T(8,128)(2,1)} async-done(((bf16[4096,512]{0,1:T(8,128)(2,1)}), bf16[512,512]{0,1:T(8,128)(2,1)}) %reduce-scatter.2.cloned.1.call-update) | async-done | bytes 524304 | tf_op jit(solution)/shard_map/reduce_scatter | solution.py:139
  136.6 1.2 convert_element_type.49
  137.8 2.5 %collective-permute-start.8 = (f32[256,512]{0,1:T(8,128)S(1)}, f32[256,512]{0,1:T(8,128)S(1)}, u32[]{:S(2)}, u32[]{:S(2)}) collective-permute-start(f32[256,512]{0,1:T(8,128)S(1)} %slice_select_fusion), channel_id=1, source_target_pairs={{0,64},{64,0},{1,65},{65,1},{2,66},{66,2},{3,67},{67,3},{4,68},{68... | collective-permute-start | bytes 1572872 | tf_op jit(solution)/shard_map/ppermute | solution.py:144
  140.4 6.0 %collective-permute-start.6 = (f32[128,256]{0,1:T(8,128)S(1)}, f32[128,256]{0,1:T(8,128)}, u32[]{:S(2)}, u32[]{:S(2)}) collective-permute-start(f32[128,256]{0,1:T(8,128)S(1)} %pad_maximum_fusion.2), channel_id=1, source_target_pairs={{3,0},{4,1},{5,2},{6,3},{7,4},{64,5},{65,6},{66,7},{67,64},{68,65}... | collective-permute-start | bytes 393224 | tf_op jit(solution)/shard_map/ppermute | solution.py:17
  147.8 2.2 %collective-permute-start.9 = (f32[256,256]{1,0:T(8,128)S(1)}, f32[256,256]{1,0:T(8,128)S(1)}, u32[]{:S(2)}, u32[]{:S(2)}) collective-permute-start(f32[256,256]{1,0:T(8,128)S(1)} %bitcast.142), channel_id=1, source_target_pairs={{0,1},{1,0},{2,3},{3,2},{4,5},{5,4},{6,7},{7,6},{8,9},{9,8},{10,11... | collective-permute-start | bytes 786440 | tf_op jit(solution)/shard_map/ppermute | solution.py:34
  150.1 4.5 %collective-permute-start.7 = (f32[128,256]{0,1:T(8,128)S(1)}, f32[128,256]{0,1:T(8,128)S(1)}, u32[]{:S(2)}, u32[]{:S(2)}) collective-permute-start(f32[128,256]{0,1:T(8,128)S(1)} %pad_maximum_fusion.3), channel_id=1, source_target_pairs={{4,0},{5,1},{6,2},{7,3},{64,4},{65,5},{66,6},{67,7},{68,64},{69,65... | collective-permute-start | bytes 393224 | tf_op jit(solution)/shard_map/ppermute | solution.py:17
  155.5 2.2 %collective-permute-done.9 = f32[256,256]{1,0:T(8,128)S(1)} collective-permute-done((f32[256,256]{1,0:T(8,128)S(1)}, f32[256,256]{1,0:T(8,128)S(1)}, u32[]{:S(2)}, u32[]{:S(2)}) %collective-permute-start.9) | collective-permute-done | bytes 262176 | tf_op jit(solution)/shard_map/ppermute | solution.py:34
  157.8 5.0 %collective-permute-start.10 = (f32[128,256]{1,0:T(8,128)S(1)}, f32[128,256]{1,0:T(8,128)S(1)}, u32[]{:S(2)}, u32[]{:S(2)}) collective-permute-start(f32[128,256]{1,0:T(8,128)S(1)} %slice_select_fusion.3), channel_id=1, source_target_pairs={{0,2},{1,3},{2,0},{3,1},{4,6},{5,7},{6,4},{7,5},{8,10},{9,11},{10,... | collective-permute-start | bytes 393224 | tf_op jit(solution)/shard_map/ppermute | solution.py:34
  164.6 7.2 %collective-permute-done.10 = f32[128,256]{1,0:T(8,128)S(1)} collective-permute-done((f32[128,256]{1,0:T(8,128)S(1)}, f32[128,256]{1,0:T(8,128)S(1)}, u32[]{:S(2)}, u32[]{:S(2)}) %collective-permute-start.10) | collective-permute-done | bytes 131104 | tf_op jit(solution)/shard_map/ppermute | solution.py:34
  171.8 3.5 %collective-permute-start.11 = (f32[64,256]{1,0:T(8,128)S(1)}, f32[64,256]{1,0:T(8,128)S(1)}, u32[]{:S(2)}, u32[]{:S(2)}) collective-permute-start(f32[64,256]{1,0:T(8,128)S(1)} %slice_select_fusion.4), channel_id=1, source_target_pairs={{0,4},{1,5},{2,6},{3,7},{4,0},{5,1},{6,2},{7,3},{8,12},{9,13},{10,... | collective-permute-start | bytes 196616 | tf_op jit(solution)/shard_map/ppermute | solution.py:34
  176.0 6.2 %collective-permute-done.11 = f32[64,256]{1,0:T(8,128)S(1)} collective-permute-done((f32[64,256]{1,0:T(8,128)S(1)}, f32[64,256]{1,0:T(8,128)S(1)}, u32[]{:S(2)}, u32[]{:S(2)}) %collective-permute-start.11) | collective-permute-done | bytes 65568 | tf_op jit(solution)/shard_map/ppermute | solution.py:34
  (77 shorter events, 14.2 us)
Async XLA Ops:
  7.2 58.3 %all-gather.2.cloned.1.call-start = ((), (), s32[]{:S(2)}) async-start(), calls=%async_computation.1 | async-start | bytes 2359296 | tf_op jit(solution)/shard_map/all_gather | solution.py:108
  7.9 128.7 %reduce-scatter.2.cloned.1.call-start = ((), (), s32[]{:S(2)}) async-start(), calls=%async_computation.2 | async-start | bytes 4718592 | tf_op jit(solution)/shard_map/reduce_scatter | solution.py:139
  9.5 23.0 %collective-permute-start = (bf16[128,256]{1,0:T(8,128)(2,1)S(1)}, bf16[128,256]{1,0:T(8,128)(2,1)S(1)}, u32[]{:S(2)}, u32[]{:S(2)}) collective-permute-start(bf16[128,256]{1,0:T(8,128)(2,1)S(1)} %pad_maximum_fusion.4), channel_id=1, source_target_pairs={{0,1},{1,2},{2,3},{3,4},{4,5},{5,6},{6,7},{7,64},{64,65},{65,66},{... | collective-permute-start | bytes 196616 | tf_op jit(solution)/shard_map/ppermute | solution.py:17
  13.4 19.1 %collective-permute-start.1 = (bf16[128,256]{1,0:T(8,128)(2,1)S(1)}, bf16[128,256]{1,0:T(8,128)(2,1)S(1)}, u32[]{:S(2)}, u32[]{:S(2)}) collective-permute-start(bf16[128,256]{1,0:T(8,128)(2,1)S(1)} %pad_maximum_fusion.4), channel_id=1, source_target_pairs={{0,2},{1,3},{2,4},{3,5},{4,6},{5,7},{6,64},{7,65},{64,66},{65,67},... | collective-permute-start | bytes 196616 | tf_op jit(solution)/shard_map/ppermute | solution.py:17
  17.5 15.0 %collective-permute-start.2 = (bf16[128,256]{1,0:T(8,128)(2,1)S(1)}, bf16[128,256]{1,0:T(8,128)(2,1)S(1)}, u32[]{:S(2)}, u32[]{:S(2)}) collective-permute-start(bf16[128,256]{1,0:T(8,128)(2,1)S(1)} %pad_maximum_fusion.4), channel_id=1, source_target_pairs={{0,3},{1,4},{2,5},{3,6},{4,7},{5,64},{6,65},{7,66},{64,67},{65,68}... | collective-permute-start | bytes 196616 | tf_op jit(solution)/shard_map/ppermute | solution.py:17
  21.9 10.7 %collective-permute-start.3 = (bf16[128,256]{1,0:T(8,128)(2,1)S(1)}, bf16[128,256]{1,0:T(8,128)(2,1)S(1)}, u32[]{:S(2)}, u32[]{:S(2)}) collective-permute-start(bf16[128,256]{1,0:T(8,128)(2,1)S(1)} %pad_maximum_fusion.4), channel_id=1, source_target_pairs={{0,4},{1,5},{2,6},{3,7},{4,64},{5,65},{6,66},{7,67},{64,68},{65,69... | collective-permute-start | bytes 196616 | tf_op jit(solution)/shard_map/ppermute | solution.py:17
  31.5 2.6 %copy-start.1 = (pred[256,768]{0,1:T(8,128)(4,1)}, pred[256,768]{0,1:T(8,128)(4,1)S(1)}, u32[]{:S(2)}) copy-start(pred[256,768]{0,1:T(8,128)(4,1)S(1)} %pad_add_fusion) | copy-start | bytes 589828
  32.6 0.7 copy-start.3
  32.6 1.5 copy-start.7
  34.1 45.1 %copy-start = (f32[768,256,4]{1,0,2:T(8,128)}, f32[768,256,4]{1,0,2:T(8,128)S(1)}, u32[]{:S(2)}) copy-start(f32[768,256,4]{1,0,2:T(8,128)S(1)} %get-tuple-element.37) | copy-start | bytes 9437188
  77.1 2.1 %copy-start.2 = (pred[256,768]{0,1:T(8,128)(4,1)S(1)}, pred[256,768]{0,1:T(8,128)(4,1)}, u32[]{:S(2)}) copy-start(pred[256,768]{0,1:T(8,128)(4,1)} %copy-done.1) | copy-start | bytes 589828
  77.1 2.1 %copy-start.6 = (bf16[256,512]{0,1:T(8,128)(2,1)S(1)}, bf16[256,512]{0,1:T(8,128)(2,1)}, u32[]{:S(2)}) copy-start(bf16[256,512]{0,1:T(8,128)(2,1)} %copy.50) | copy-start | bytes 786436
  77.1 2.1 %copy-start.8 = (bf16[768,128]{1,0:T(8,128)(2,1)S(1)}, bf16[768,128]{1,0:T(8,128)(2,1)}, u32[]{:S(2)}) copy-start(bf16[768,128]{1,0:T(8,128)(2,1)} %copy-done.7) | copy-start | bytes 589828
  79.2 1.1 copy-start.5
  83.1 64.2 %copy-start.4 = (bf16[768,128]{1,0:T(8,128)(2,1)S(1)}, bf16[768,128]{1,0:T(8,128)(2,1)}, u32[]{:S(2)}) copy-start(bf16[768,128]{1,0:T(8,128)(2,1)} %copy-done.3) | copy-start | bytes 589828
  83.8 79.0 %collective-permute-start.4 = (f32[128,256]{0,1:T(8,128)S(1)}, f32[128,256]{0,1:T(8,128)S(1)}, u32[]{:S(2)}, u32[]{:S(2)}) collective-permute-start(f32[128,256]{0,1:T(8,128)S(1)} %pad_maximum_fusion), channel_id=1, source_target_pairs={{1,0},{2,1},{3,2},{4,3},{5,4},{6,5},{7,6},{64,7},{65,64},{66,65},{... | collective-permute-start | bytes 393224 | tf_op jit(solution)/shard_map/ppermute | solution.py:17
  92.4 70.5 %collective-permute-start.5 = (f32[128,256]{0,1:T(8,128)S(1)}, f32[128,256]{0,1:T(8,128)S(1)}, u32[]{:S(2)}, u32[]{:S(2)}) collective-permute-start(f32[128,256]{0,1:T(8,128)S(1)} %pad_maximum_fusion.1), channel_id=1, source_target_pairs={{2,0},{3,1},{4,2},{5,3},{6,4},{7,5},{64,6},{65,7},{66,64},{67,65},... | collective-permute-start | bytes 393224 | tf_op jit(solution)/shard_map/ppermute | solution.py:17
  137.8 9.8 %collective-permute-start.8 = (f32[256,512]{0,1:T(8,128)S(1)}, f32[256,512]{0,1:T(8,128)S(1)}, u32[]{:S(2)}, u32[]{:S(2)}) collective-permute-start(f32[256,512]{0,1:T(8,128)S(1)} %slice_select_fusion), channel_id=1, source_target_pairs={{0,64},{64,0},{1,65},{65,1},{2,66},{66,2},{3,67},{67,3},{4,68},{68... | collective-permute-start | bytes 1572872 | tf_op jit(solution)/shard_map/ppermute | solution.py:144
  140.4 22.5 %collective-permute-start.6 = (f32[128,256]{0,1:T(8,128)S(1)}, f32[128,256]{0,1:T(8,128)}, u32[]{:S(2)}, u32[]{:S(2)}) collective-permute-start(f32[128,256]{0,1:T(8,128)S(1)} %pad_maximum_fusion.2), channel_id=1, source_target_pairs={{3,0},{4,1},{5,2},{6,3},{7,4},{64,5},{65,6},{66,7},{67,64},{68,65}... | collective-permute-start | bytes 393224 | tf_op jit(solution)/shard_map/ppermute | solution.py:17
  147.8 9.9 %collective-permute-start.9 = (f32[256,256]{1,0:T(8,128)S(1)}, f32[256,256]{1,0:T(8,128)S(1)}, u32[]{:S(2)}, u32[]{:S(2)}) collective-permute-start(f32[256,256]{1,0:T(8,128)S(1)} %bitcast.142), channel_id=1, source_target_pairs={{0,1},{1,0},{2,3},{3,2},{4,5},{5,4},{6,7},{7,6},{8,9},{9,8},{10,11... | collective-permute-start | bytes 786440 | tf_op jit(solution)/shard_map/ppermute | solution.py:34
  150.1 12.8 %collective-permute-start.7 = (f32[128,256]{0,1:T(8,128)S(1)}, f32[128,256]{0,1:T(8,128)S(1)}, u32[]{:S(2)}, u32[]{:S(2)}) collective-permute-start(f32[128,256]{0,1:T(8,128)S(1)} %pad_maximum_fusion.3), channel_id=1, source_target_pairs={{4,0},{5,1},{6,2},{7,3},{64,4},{65,5},{66,6},{67,7},{68,64},{69,65... | collective-permute-start | bytes 393224 | tf_op jit(solution)/shard_map/ppermute | solution.py:17
  157.8 13.9 %collective-permute-start.10 = (f32[128,256]{1,0:T(8,128)S(1)}, f32[128,256]{1,0:T(8,128)S(1)}, u32[]{:S(2)}, u32[]{:S(2)}) collective-permute-start(f32[128,256]{1,0:T(8,128)S(1)} %slice_select_fusion.3), channel_id=1, source_target_pairs={{0,2},{1,3},{2,0},{3,1},{4,6},{5,7},{6,4},{7,5},{8,10},{9,11},{10,... | collective-permute-start | bytes 393224 | tf_op jit(solution)/shard_map/ppermute | solution.py:34
  171.8 10.4 %collective-permute-start.11 = (f32[64,256]{1,0:T(8,128)S(1)}, f32[64,256]{1,0:T(8,128)S(1)}, u32[]{:S(2)}, u32[]{:S(2)}) collective-permute-start(f32[64,256]{1,0:T(8,128)S(1)} %slice_select_fusion.4), channel_id=1, source_target_pairs={{0,4},{1,5},{2,6},{3,7},{4,0},{5,1},{6,2},{7,3},{8,12},{9,13},{10,... | collective-permute-start | bytes 196616 | tf_op jit(solution)/shard_map/ppermute | solution.py:34
Sparse Core Ops, SparseCore 0:
  10.7 54.7 all-gather.1
  70.5 65.9 reduce-scatter.1

commit v3 on v2

--- a/solution.py
+++ b/solution.py
@@ -137,6 +137,7 @@
         grad_rows, attended, (((0,), (0,)), ((), ())), preferred_element_type=jnp.float32
     ).astype(jnp.bfloat16)
     chip_cols = lax.psum_scatter(term, "z", scatter_dimension=0, tiled=True).astype(jnp.float32)
+    chip_cols, d_keys, d_values = lax.optimization_barrier((chip_cols, d_keys, d_values))
     half = chip_cols.shape[0] // 2
     upper = lax.axis_index("core") == 1
     kept = jnp.where(upper, chip_cols[half:], chip_cols[:half])

time: 191 us -> 183 us (0.958)
  the two profiles are of different devices: /device:TPU:1 before, /device:TPU:14 now
where the time goes in v3:
time: 183 us; the launch traced here: 182 us
  waiting for transfers between devices  97.4 us (53%)
  starting transfers between devices  38.6 us (21%)
  matrix products  16.3 us (9%)
  between operations  14.6 us (8%)
  local copies, waits for them, and re-layouts  8.53 us (5%)
  other arithmetic  6.84 us (4%)
    all_gather x1, waiting for transfers between devices, local(): grad_rows = lax.all_gather(out_grad, 'head', axis=1, tiled=True)  33.8 us
    ppermute x8, starting transfers between devices, passed_along(): return lax.ppermute(x, axis, pairs)  29.6 us
    reduce_scatter x1, waiting for transfers between devices, local(): lax.psum_scatter(term, 'z', scatter_dimension=0, tiled=True)  27.3 us
    ppermute x3, waiting for transfers between devices, exchange_sum(): lax.ppermute(give, axis, [(i, i ^ span) for i in range(peers)])  20.7 us
    ppermute x8, waiting for transfers between devices, passed_along(): return lax.ppermute(x, axis, pairs)  12.7 us
    ppermute x3, starting transfers between devices, exchange_sum(): lax.ppermute(give, axis, [(i, i ^ span) for i in range(peers)])  6.96 us
    dot_general x1, matrix products, local(): lax.dot_general(grad_rows, attended, (((0,), (0,)), ((), ())), preferred_...  4.89 us
    dot_general x1, matrix products, local(): lax.dot_general(grad_rows, out_proj, (((1,), (1,)), ((), ())), preferred_...  4.82 us
  transfers between devices with their start and end apart: 14, of which 10 were waited for; matrix products, arithmetic and copies ran while one was open for 13% of the time, Pallas kernels for 0%

profile of v3, /device:TPU:14, one launch (start us, length us, event | category | flops | bytes accessed | tf_op | source)
XLA Modules:
  0.0 182.3 jit_solution(13009326286095776551)
XLA Ops:
  9.5 1.9 %collective-permute-start = (bf16[128,256]{1,0:T(8,128)(2,1)S(1)}, bf16[128,256]{1,0:T(8,128)(2,1)S(1)}, u32[]{:S(2)}, u32[]{:S(2)}) collective-permute-start(bf16[128,256]{1,0:T(8,128)(2,1)S(1)} %pad_maximum_fusion.4), channel_id=1, source_target_pairs={{0,1},{1,2},{2,3},{3,4},{4,5},{5,6},{6,7},{7,64},{64,65},{65,66},{... | collective-permute-start | bytes 196616 | tf_op jit(solution)/shard_map/ppermute | solution.py:17
  11.4 3.8 %collective-permute-start.1 = (bf16[128,256]{1,0:T(8,128)(2,1)S(1)}, bf16[128,256]{1,0:T(8,128)(2,1)S(1)}, u32[]{:S(2)}, u32[]{:S(2)}) collective-permute-start(bf16[128,256]{1,0:T(8,128)(2,1)S(1)} %pad_maximum_fusion.4), channel_id=1, source_target_pairs={{0,2},{1,3},{2,4},{3,5},{4,6},{5,7},{6,64},{7,65},{64,66},{65,67},... | collective-permute-start | bytes 196616 | tf_op jit(solution)/shard_map/ppermute | solution.py:17
  15.3 5.3 %collective-permute-start.2 = (bf16[128,256]{1,0:T(8,128)(2,1)S(1)}, bf16[128,256]{1,0:T(8,128)(2,1)S(1)}, u32[]{:S(2)}, u32[]{:S(2)}) collective-permute-start(bf16[128,256]{1,0:T(8,128)(2,1)S(1)} %pad_maximum_fusion.4), channel_id=1, source_target_pairs={{0,3},{1,4},{2,5},{3,6},{4,7},{5,64},{6,65},{7,66},{64,67},{65,68}... | collective-permute-start | bytes 196616 | tf_op jit(solution)/shard_map/ppermute | solution.py:17
  20.5 6.5 %collective-permute-start.3 = (bf16[128,256]{1,0:T(8,128)(2,1)S(1)}, bf16[128,256]{1,0:T(8,128)(2,1)S(1)}, u32[]{:S(2)}, u32[]{:S(2)}) collective-permute-start(bf16[128,256]{1,0:T(8,128)(2,1)S(1)} %pad_maximum_fusion.4), channel_id=1, source_target_pairs={{0,4},{1,5},{2,6},{3,7},{4,64},{5,65},{6,66},{7,67},{64,68},{65,69... | collective-permute-start | bytes 196616 | tf_op jit(solution)/shard_map/ppermute | solution.py:17
  34.4 33.8 %all-gather.2.cloned.1.call-done = bf16[256,4096]{1,0:T(8,128)(2,1)} async-done(((bf16[256,512]{1,0:T(8,128)(2,1)}), bf16[256,4096]{1,0:T(8,128)(2,1)}) %all-gather.2.cloned.1.call-update) | async-done | bytes 2097168 | tf_op jit(solution)/shard_map/all_gather | solution.py:108
  68.2 4.9 %fusion = bf16[4096,512]{0,1:T(8,128)(2,1)} fusion(bf16[256,512]{0,1:T(8,128)(2,1)} %bitcast.141, bf16[256,4096]{1,0:T(8,128)(2,1)} %all-gather.2.cloned.1.call-done), kind=kOutput, calls=%fused_computation.1 | convolution fusion | flops 1075838976 | bytes 6553600 | tf_op jit(solution)/shard_map/dot_general | solution.py:136
  73.1 4.8 %convolution_convert_fusion.2 = bf16[256,512]{1,0:T(8,128)(2,1)} fusion(bf16[256,4096]{1,0:T(8,128)(2,1)} %all-gather.2.cloned.1.call-done, bf16[512,4096]{1,0:T(8,128)(2,1)} %param.11), kind=kOutput, calls=%fused_computation.21 | convolution fusion | flops 1073872896 | bytes 6553600 | tf_op jit(solution)/shard_map/dot_general | solution.py:109
  79.7 2.0 %fusion.16 = f32[768,1,128]{0,2,1:T(8,128)S(1)} fusion(bf16[256,4,128]{0,2,1:T(8,128)(2,1)} %bitcast.143, f32[4,256]{1,0:T(4,128)S(1)} %get-tuple-element.42, f32[768,256,4]{1,0,2:T(8,128)S(1)} %get-tuple-element.43, pred[256,768]{0,1:T(8,128)(4,1)} %copy-done.1), kind=kOutput, calls=%fused_computation.18 | convolution fusion | flops 204472320 | bytes 4001792 | tf_op jit(solution)/shard_map/kgst,skgd->tkd/dot_general | solution.py:86
  82.8 2.8 %fusion.7 = bf16[4,256,768]{1,2,0:T(8,128)(2,1)S(1)} fusion(f32[768,256,4]{1,0,2:T(8,128)S(1)} %get-tuple-element.45, f32[4,256]{1,0:T(4,128)S(1)} %get-tuple-element.44, f32[4,256]{1,0:T(4,128)S(1)} %get-tuple-element.42, f32[768,256,4]{1,0,2:T(8,128)} %copy-done, pred[256,768]{0,1:T(8,128)(4,1)S(1)} %copy-done.2), kind=kLoop, calls=%fused_computation.11 | loop fusion | flops 5505024 | bytes 8069120 | tf_op jit(solution)/shard_map/reshape.9
  86.3 3.4 %collective-permute-start.4 = (f32[128,256]{0,1:T(8,128)S(1)}, f32[128,256]{0,1:T(8,128)S(1)}, u32[]{:S(2)}, u32[]{:S(2)}) collective-permute-start(f32[128,256]{0,1:T(8,128)S(1)} %pad_maximum_fusion), channel_id=1, source_target_pairs={{1,0},{2,1},{3,2},{4,3},{5,4},{6,5},{7,6},{64,7},{65,64},{66,65},{... | collective-permute-start | bytes 393224 | tf_op jit(solution)/shard_map/ppermute | solution.py:17
  89.7 4.2 %collective-permute-start.5 = (f32[128,256]{0,1:T(8,128)S(1)}, f32[128,256]{0,1:T(8,128)S(1)}, u32[]{:S(2)}, u32[]{:S(2)}) collective-permute-start(f32[128,256]{0,1:T(8,128)S(1)} %pad_maximum_fusion.1), channel_id=1, source_target_pairs={{2,0},{3,1},{4,2},{5,3},{6,4},{7,5},{64,6},{65,7},{66,64},{67,65},... | collective-permute-start | bytes 393224 | tf_op jit(solution)/shard_map/ppermute | solution.py:17
  94.0 2.5 %collective-permute-start.6 = (f32[128,256]{0,1:T(8,128)S(1)}, f32[128,256]{0,1:T(8,128)S(1)}, u32[]{:S(2)}, u32[]{:S(2)}) collective-permute-start(f32[128,256]{0,1:T(8,128)S(1)} %pad_maximum_fusion.2), channel_id=1, source_target_pairs={{3,0},{4,1},{5,2},{6,3},{7,4},{64,5},{65,6},{66,7},{67,64},{68,65}... | collective-permute-start | bytes 393224 | tf_op jit(solution)/shard_map/ppermute | solution.py:17
  98.5 2.5 %collective-permute-done.5 = f32[128,256]{0,1:T(8,128)S(1)} collective-permute-done((f32[128,256]{0,1:T(8,128)S(1)}, f32[128,256]{0,1:T(8,128)S(1)}, u32[]{:S(2)}, u32[]{:S(2)}) %collective-permute-start.5) | collective-permute-done | bytes 131104 | tf_op jit(solution)/shard_map/ppermute | solution.py:17
  101.0 4.9 %collective-permute-done.6 = f32[128,256]{0,1:T(8,128)S(1)} collective-permute-done((f32[128,256]{0,1:T(8,128)S(1)}, f32[128,256]{0,1:T(8,128)S(1)}, u32[]{:S(2)}, u32[]{:S(2)}) %collective-permute-start.6) | collective-permute-done | bytes 131104 | tf_op jit(solution)/shard_map/ppermute | solution.py:17
  106.0 4.4 %collective-permute-done.7 = f32[128,256]{0,1:T(8,128)S(1)} collective-permute-done((f32[128,256]{0,1:T(8,128)S(1)}, f32[128,256]{0,1:T(8,128)S(1)}, u32[]{:S(2)}, u32[]{:S(2)}) %collective-permute-start.7) | collective-permute-done | bytes 131104 | tf_op jit(solution)/shard_map/ppermute | solution.py:17
  110.5 27.3 %reduce-scatter.2.cloned.1.call-done = bf16[512,512]{0,1:T(8,128)(2,1)} async-done(((bf16[4096,512]{0,1:T(8,128)(2,1)}), bf16[512,512]{0,1:T(8,128)(2,1)}) %reduce-scatter.2.cloned.1.call-update) | async-done | bytes 524304 | tf_op jit(solution)/shard_map/reduce_scatter | solution.py:139
  139.8 2.0 %collective-permute-start.8 = (f32[256,512]{0,1:T(8,128)}, f32[256,512]{0,1:T(8,128)S(1)}, u32[]{:S(2)}, u32[]{:S(2)}) collective-permute-start(f32[256,512]{0,1:T(8,128)} %slice_select_fusion), channel_id=1, source_target_pairs={{0,64},{64,0},{1,65},{65,1},{2,66},{66,2},{3,67},{67,3},{4,68},{68... | collective-permute-start | bytes 1572872 | tf_op jit(solution)/shard_map/ppermute | solution.py:145
  141.9 2.1 %collective-permute-done.8 = f32[256,512]{0,1:T(8,128)S(1)} collective-permute-done((f32[256,512]{0,1:T(8,128)}, f32[256,512]{0,1:T(8,128)S(1)}, u32[]{:S(2)}, u32[]{:S(2)}) %collective-permute-start.8) | collective-permute-done | bytes 524320 | tf_op jit(solution)/shard_map/ppermute | solution.py:145
  144.2 2.0 %collective-permute-start.9 = (f32[256,256]{1,0:T(8,128)S(1)}, f32[256,256]{1,0:T(8,128)S(1)}, u32[]{:S(2)}, u32[]{:S(2)}) collective-permute-start(f32[256,256]{1,0:T(8,128)S(1)} %bitcast.142), channel_id=1, source_target_pairs={{0,1},{1,0},{2,3},{3,2},{4,5},{5,4},{6,7},{7,6},{8,9},{9,8},{10,11... | collective-permute-start | bytes 786440 | tf_op jit(solution)/shard_map/ppermute | solution.py:34
  146.2 8.2 %collective-permute-done.9 = f32[256,256]{1,0:T(8,128)S(1)} collective-permute-done((f32[256,256]{1,0:T(8,128)S(1)}, f32[256,256]{1,0:T(8,128)S(1)}, u32[]{:S(2)}, u32[]{:S(2)}) %collective-permute-start.9) | collective-permute-done | bytes 262176 | tf_op jit(solution)/shard_map/ppermute | solution.py:34
  154.5 2.0 %collective-permute-start.10 = (f32[128,256]{1,0:T(8,128)S(1)}, f32[128,256]{1,0:T(8,128)S(1)}, u32[]{:S(2)}, u32[]{:S(2)}) collective-permute-start(f32[128,256]{1,0:T(8,128)S(1)} %slice_select_fusion.3), channel_id=1, source_target_pairs={{0,2},{1,3},{2,0},{3,1},{4,6},{5,7},{6,4},{7,5},{8,10},{9,11},{10,... | collective-permute-start | bytes 393224 | tf_op jit(solution)/shard_map/ppermute | solution.py:34
  156.5 8.2 %collective-permute-done.10 = f32[128,256]{1,0:T(8,128)S(1)} collective-permute-done((f32[128,256]{1,0:T(8,128)S(1)}, f32[128,256]{1,0:T(8,128)S(1)}, u32[]{:S(2)}, u32[]{:S(2)}) %collective-permute-start.10) | collective-permute-done | bytes 131104 | tf_op jit(solution)/shard_map/ppermute | solution.py:34
  164.7 2.9 %collective-permute-start.11 = (f32[64,256]{1,0:T(8,128)S(1)}, f32[64,256]{1,0:T(8,128)S(1)}, u32[]{:S(2)}, u32[]{:S(2)}) collective-permute-start(f32[64,256]{1,0:T(8,128)S(1)} %slice_select_fusion.4), channel_id=1, source_target_pairs={{0,4},{1,5},{2,6},{3,7},{4,0},{5,1},{6,2},{7,3},{8,12},{9,13},{10,... | collective-permute-start | bytes 196616 | tf_op jit(solution)/shard_map/ppermute | solution.py:34
  170.4 4.4 %collective-permute-done.11 = f32[64,256]{1,0:T(8,128)S(1)} collective-permute-done((f32[64,256]{1,0:T(8,128)S(1)}, f32[64,256]{1,0:T(8,128)S(1)}, u32[]{:S(2)}, u32[]{:S(2)}) %collective-permute-start.11) | collective-permute-done | bytes 65568 | tf_op jit(solution)/shard_map/ppermute | solution.py:34
  (75 shorter events, 20.6 us)
Async XLA Ops:
  7.2 61.0 %all-gather.2.cloned.1.call-start = ((), (), s32[]{:S(2)}) async-start(), calls=%async_computation.1 | async-start | bytes 2359296 | tf_op jit(solution)/shard_map/all_gather | solution.py:108
  7.9 129.9 %reduce-scatter.2.cloned.1.call-start = ((), (), s32[]{:S(2)}) async-start(), calls=%async_computation.2 | async-start | bytes 4718592 | tf_op jit(solution)/shard_map/reduce_scatter | solution.py:139
  9.5 20.8 %collective-permute-start = (bf16[128,256]{1,0:T(8,128)(2,1)S(1)}, bf16[128,256]{1,0:T(8,128)(2,1)S(1)}, u32[]{:S(2)}, u32[]{:S(2)}) collective-permute-start(bf16[128,256]{1,0:T(8,128)(2,1)S(1)} %pad_maximum_fusion.4), channel_id=1, source_target_pairs={{0,1},{1,2},{2,3},{3,4},{4,5},{5,6},{6,7},{7,64},{64,65},{65,66},{... | collective-permute-start | bytes 196616 | tf_op jit(solution)/shard_map/ppermute | solution.py:17
  11.4 18.9 %collective-permute-start.1 = (bf16[128,256]{1,0:T(8,128)(2,1)S(1)}, bf16[128,256]{1,0:T(8,128)(2,1)S(1)}, u32[]{:S(2)}, u32[]{:S(2)}) collective-permute-start(bf16[128,256]{1,0:T(8,128)(2,1)S(1)} %pad_maximum_fusion.4), channel_id=1, source_target_pairs={{0,2},{1,3},{2,4},{3,5},{4,6},{5,7},{6,64},{7,65},{64,66},{65,67},... | collective-permute-start | bytes 196616 | tf_op jit(solution)/shard_map/ppermute | solution.py:17
  15.3 15.0 %collective-permute-start.2 = (bf16[128,256]{1,0:T(8,128)(2,1)S(1)}, bf16[128,256]{1,0:T(8,128)(2,1)S(1)}, u32[]{:S(2)}, u32[]{:S(2)}) collective-permute-start(bf16[128,256]{1,0:T(8,128)(2,1)S(1)} %pad_maximum_fusion.4), channel_id=1, source_target_pairs={{0,3},{1,4},{2,5},{3,6},{4,7},{5,64},{6,65},{7,66},{64,67},{65,68}... | collective-permute-start | bytes 196616 | tf_op jit(solution)/shard_map/ppermute | solution.py:17
  20.5 10.6 %collective-permute-start.3 = (bf16[128,256]{1,0:T(8,128)(2,1)S(1)}, bf16[128,256]{1,0:T(8,128)(2,1)S(1)}, u32[]{:S(2)}, u32[]{:S(2)}) collective-permute-start(bf16[128,256]{1,0:T(8,128)(2,1)S(1)} %pad_maximum_fusion.4), channel_id=1, source_target_pairs={{0,4},{1,5},{2,6},{3,7},{4,64},{5,65},{6,66},{7,67},{64,68},{65,69... | collective-permute-start | bytes 196616 | tf_op jit(solution)/shard_map/ppermute | solution.py:17
  29.3 3.4 %copy-start.1 = (pred[256,768]{0,1:T(8,128)(4,1)}, pred[256,768]{0,1:T(8,128)(4,1)S(1)}, u32[]{:S(2)}) copy-start(pred[256,768]{0,1:T(8,128)(4,1)S(1)} %pad_add_fusion) | copy-start | bytes 589828
  31.1 0.7 copy-start.3
  31.2 1.5 copy-start.6
  32.6 49.1 %copy-start = (f32[768,256,4]{1,0,2:T(8,128)}, f32[768,256,4]{1,0,2:T(8,128)S(1)}, u32[]{:S(2)}) copy-start(f32[768,256,4]{1,0,2:T(8,128)S(1)} %get-tuple-element.43) | copy-start | bytes 9437188
  79.7 2.1 %copy-start.2 = (pred[256,768]{0,1:T(8,128)(4,1)S(1)}, pred[256,768]{0,1:T(8,128)(4,1)}, u32[]{:S(2)}) copy-start(pred[256,768]{0,1:T(8,128)(4,1)} %copy-done.1) | copy-start | bytes 589828
  79.7 2.1 %copy-start.5 = (bf16[256,512]{0,1:T(8,128)(2,1)S(1)}, bf16[256,512]{0,1:T(8,128)(2,1)}, u32[]{:S(2)}) copy-start(bf16[256,512]{0,1:T(8,128)(2,1)} %copy.50) | copy-start | bytes 786436
  79.7 2.1 %copy-start.7 = (bf16[768,128]{1,0:T(8,128)(2,1)S(1)}, bf16[768,128]{1,0:T(8,128)(2,1)}, u32[]{:S(2)}) copy-start(bf16[768,128]{1,0:T(8,128)(2,1)} %copy-done.6) | copy-start | bytes 589828
  86.3 12.1 %collective-permute-start.4 = (f32[128,256]{0,1:T(8,128)S(1)}, f32[128,256]{0,1:T(8,128)S(1)}, u32[]{:S(2)}, u32[]{:S(2)}) collective-permute-start(f32[128,256]{0,1:T(8,128)S(1)} %pad_maximum_fusion), channel_id=1, source_target_pairs={{1,0},{2,1},{3,2},{4,3},{5,4},{6,5},{7,6},{64,7},{65,64},{66,65},{... | collective-permute-start | bytes 393224 | tf_op jit(solution)/shard_map/ppermute | solution.py:17
  89.7 11.3 %collective-permute-start.5 = (f32[128,256]{0,1:T(8,128)S(1)}, f32[128,256]{0,1:T(8,128)S(1)}, u32[]{:S(2)}, u32[]{:S(2)}) collective-permute-start(f32[128,256]{0,1:T(8,128)S(1)} %pad_maximum_fusion.1), channel_id=1, source_target_pairs={{2,0},{3,1},{4,2},{5,3},{6,4},{7,5},{64,6},{65,7},{66,64},{67,65},... | collective-permute-start | bytes 393224 | tf_op jit(solution)/shard_map/ppermute | solution.py:17
  94.0 12.0 %collective-permute-start.6 = (f32[128,256]{0,1:T(8,128)S(1)}, f32[128,256]{0,1:T(8,128)S(1)}, u32[]{:S(2)}, u32[]{:S(2)}) collective-permute-start(f32[128,256]{0,1:T(8,128)S(1)} %pad_maximum_fusion.2), channel_id=1, source_target_pairs={{3,0},{4,1},{5,2},{6,3},{7,4},{64,5},{65,6},{66,7},{67,64},{68,65}... | collective-permute-start | bytes 393224 | tf_op jit(solution)/shard_map/ppermute | solution.py:17
  96.5 13.9 %collective-permute-start.7 = (f32[128,256]{0,1:T(8,128)S(1)}, f32[128,256]{0,1:T(8,128)S(1)}, u32[]{:S(2)}, u32[]{:S(2)}) collective-permute-start(f32[128,256]{0,1:T(8,128)S(1)} %pad_maximum_fusion.3), channel_id=1, source_target_pairs={{4,0},{5,1},{6,2},{7,3},{64,4},{65,5},{66,6},{67,7},{68,64},{69,65... | collective-permute-start | bytes 393224 | tf_op jit(solution)/shard_map/ppermute | solution.py:17
  139.8 27.9 %copy-start.4 = (bf16[768,128]{1,0:T(8,128)(2,1)S(1)}, bf16[768,128]{1,0:T(8,128)(2,1)}, u32[]{:S(2)}) copy-start(bf16[768,128]{1,0:T(8,128)(2,1)} %copy-done.3) | copy-start | bytes 589828
  139.8 4.1 %collective-permute-start.8 = (f32[256,512]{0,1:T(8,128)}, f32[256,512]{0,1:T(8,128)S(1)}, u32[]{:S(2)}, u32[]{:S(2)}) collective-permute-start(f32[256,512]{0,1:T(8,128)} %slice_select_fusion), channel_id=1, source_target_pairs={{0,64},{64,0},{1,65},{65,1},{2,66},{66,2},{3,67},{67,3},{4,68},{68... | collective-permute-start | bytes 1572872 | tf_op jit(solution)/shard_map/ppermute | solution.py:145
  144.2 10.2 %collective-permute-start.9 = (f32[256,256]{1,0:T(8,128)S(1)}, f32[256,256]{1,0:T(8,128)S(1)}, u32[]{:S(2)}, u32[]{:S(2)}) collective-permute-start(f32[256,256]{1,0:T(8,128)S(1)} %bitcast.142), channel_id=1, source_target_pairs={{0,1},{1,0},{2,3},{3,2},{4,5},{5,4},{6,7},{7,6},{8,9},{9,8},{10,11... | collective-permute-start | bytes 786440 | tf_op jit(solution)/shard_map/ppermute | solution.py:34
  154.5 10.2 %collective-permute-start.10 = (f32[128,256]{1,0:T(8,128)S(1)}, f32[128,256]{1,0:T(8,128)S(1)}, u32[]{:S(2)}, u32[]{:S(2)}) collective-permute-start(f32[128,256]{1,0:T(8,128)S(1)} %slice_select_fusion.3), channel_id=1, source_target_pairs={{0,2},{1,3},{2,0},{3,1},{4,6},{5,7},{6,4},{7,5},{8,10},{9,11},{10,... | collective-permute-start | bytes 393224 | tf_op jit(solution)/shard_map/ppermute | solution.py:34
  164.7 10.1 %collective-permute-start.11 = (f32[64,256]{1,0:T(8,128)S(1)}, f32[64,256]{1,0:T(8,128)S(1)}, u32[]{:S(2)}, u32[]{:S(2)}) collective-permute-start(f32[64,256]{1,0:T(8,128)S(1)} %slice_select_fusion.4), channel_id=1, source_target_pairs={{0,4},{1,5},{2,6},{3,7},{4,0},{5,1},{6,2},{7,3},{8,12},{9,13},{10,... | collective-permute-start | bytes 196616 | tf_op jit(solution)/shard_map/ppermute | solution.py:34
Sparse Core Ops, SparseCore 0:
  10.7 57.4 all-gather.1
  73.2 64.5 reduce-scatter.1

commit v4 on v1

--- a/solution.py
+++ b/solution.py
@@ -140,6 +140,7 @@
         scatter_dimension=0,
         tiled=True,
     ).astype(jnp.float32)
+    partial_cols, d_keys, d_values = lax.optimization_barrier((partial_cols, d_keys, d_values))
     d_out_proj = exchange_sum(partial_cols.T, "dp")
     return (d_query, d_keys, d_values, d_out_proj)
 

time: 185 us -> 181 us (0.978)
  waiting for transfers between devices: 97.3 us -> 92.8 us
    reduce_scatter x1, waiting for transfers between devices: 48.3 us -> 32.7 us  [local(): lax.psum_scatter(lax.dot_general(grad_rows, attended, (((0,), (0,)), ((),...]
    ppermute x8, waiting for transfers between devices: 0.83 us -> 12.9 us  [passed_along(): return lax.ppermute(x, axis, pairs)]
    ppermute x8, starting transfers between devices: 32 us -> 29.7 us  [passed_along(): return lax.ppermute(x, axis, pairs)]
  transfers between devices with their start and end apart: 13 -> 13, of which waited for: 6 -> 9; matrix products, arithmetic and copies ran while one was open for 13% -> 13% of each run, Pallas kernels for 0% -> 0%
where the time goes in v4:
time: 181 us; the launch traced here: 180 us
  waiting for transfers between devices  92.8 us (51%)
  starting transfers between devices  42.1 us (23%)
  matrix products  16.3 us (9%)
  between operations  14.6 us (8%)
  local copies, waits for them, and re-layouts  8.52 us (5%)
  other arithmetic  5.69 us (3%)
    all_gather x1, waiting for transfers between devices, local(): grad_rows = lax.all_gather(out_grad, 'head', axis=1, tiled=True)  33.8 us
    reduce_scatter x1, waiting for transfers between devices, local(): lax.psum_scatter(lax.dot_general(grad_rows, attended, (((0,), (0,)), ((),...  32.7 us
    ppermute x8, starting transfers between devices, passed_along(): return lax.ppermute(x, axis, pairs)  29.7 us
    ppermute x8, waiting for transfers between devices, passed_along(): return lax.ppermute(x, axis, pairs)  12.9 us
    ppermute x3, waiting for transfers between devices, exchange_sum(): lax.ppermute(give, axis, [(i, i ^ span) for i in range(peers)])  12.7 us
    ppermute x3, starting transfers between devices, exchange_sum(): lax.ppermute(give, axis, [(i, i ^ span) for i in range(peers)])  12.3 us
    dot_general x1, matrix products, local(): lax.dot_general(grad_rows, attended, (((0,), (0,)), ((), ())), preferred_...  4.9 us
    dot_general x1, matrix products, local(): lax.dot_general(grad_rows, out_proj, (((1,), (1,)), ((), ())), preferred_...  4.82 us
  transfers between devices with their start and end apart: 13, of which 9 were waited for; matrix products, arithmetic and copies ran while one was open for 13% of the time, Pallas kernels for 0%

profile of v4, /device:TPU:14, one launch (start us, length us, event | category | flops | bytes accessed | tf_op | source)
XLA Modules:
  0.0 179.9 jit_solution(566040106296865530)
XLA Ops:
  9.5 1.9 %collective-permute-start = (bf16[128,256]{1,0:T(8,128)(2,1)S(1)}, bf16[128,256]{1,0:T(8,128)(2,1)S(1)}, u32[]{:S(2)}, u32[]{:S(2)}) collective-permute-start(bf16[128,256]{1,0:T(8,128)(2,1)S(1)} %pad_maximum_fusion.4), channel_id=1, source_target_pairs={{0,1},{1,2},{2,3},{3,4},{4,5},{5,6},{6,7},{7,64},{64,65},{65,66},{... | collective-permute-start | bytes 196616 | tf_op jit(solution)/shard_map/ppermute | solution.py:16
  11.4 3.8 %collective-permute-start.1 = (bf16[128,256]{1,0:T(8,128)(2,1)S(1)}, bf16[128,256]{1,0:T(8,128)(2,1)S(1)}, u32[]{:S(2)}, u32[]{:S(2)}) collective-permute-start(bf16[128,256]{1,0:T(8,128)(2,1)S(1)} %pad_maximum_fusion.4), channel_id=1, source_target_pairs={{0,2},{1,3},{2,4},{3,5},{4,6},{5,7},{6,64},{7,65},{64,66},{65,67},... | collective-permute-start | bytes 196616 | tf_op jit(solution)/shard_map/ppermute | solution.py:16
  15.3 5.3 %collective-permute-start.2 = (bf16[128,256]{1,0:T(8,128)(2,1)S(1)}, bf16[128,256]{1,0:T(8,128)(2,1)S(1)}, u32[]{:S(2)}, u32[]{:S(2)}) collective-permute-start(bf16[128,256]{1,0:T(8,128)(2,1)S(1)} %pad_maximum_fusion.4), channel_id=1, source_target_pairs={{0,3},{1,4},{2,5},{3,6},{4,7},{5,64},{6,65},{7,66},{64,67},{65,68}... | collective-permute-start | bytes 196616 | tf_op jit(solution)/shard_map/ppermute | solution.py:16
  20.5 6.5 %collective-permute-start.3 = (bf16[128,256]{1,0:T(8,128)(2,1)S(1)}, bf16[128,256]{1,0:T(8,128)(2,1)S(1)}, u32[]{:S(2)}, u32[]{:S(2)}) collective-permute-start(bf16[128,256]{1,0:T(8,128)(2,1)S(1)} %pad_maximum_fusion.4), channel_id=1, source_target_pairs={{0,4},{1,5},{2,6},{3,7},{4,64},{5,65},{6,66},{7,67},{64,68},{65,69... | collective-permute-start | bytes 196616 | tf_op jit(solution)/shard_map/ppermute | solution.py:16
  32.7 1.7 fusion.13
  34.4 33.8 %all-gather.2.cloned.1.call-done = bf16[256,4096]{1,0:T(8,128)(2,1)} async-done(((bf16[256,512]{1,0:T(8,128)(2,1)}), bf16[256,4096]{1,0:T(8,128)(2,1)}) %all-gather.2.cloned.1.call-update) | async-done | bytes 2097168 | tf_op jit(solution)/shard_map/all_gather | solution.py:107
  68.2 4.9 %fusion = bf16[4096,512]{0,1:T(8,128)(2,1)} fusion(bf16[256,512]{0,1:T(8,128)(2,1)} %bitcast.141, bf16[256,4096]{1,0:T(8,128)(2,1)} %all-gather.2.cloned.1.call-done), kind=kOutput, calls=%fused_computation.1 | convolution fusion | flops 1075838976 | bytes 6553600 | tf_op jit(solution)/shard_map/dot_general | solution.py:136
  73.1 4.8 %convolution_convert_fusion.2 = bf16[256,512]{1,0:T(8,128)(2,1)} fusion(bf16[256,4096]{1,0:T(8,128)(2,1)} %all-gather.2.cloned.1.call-done, bf16[512,4096]{1,0:T(8,128)(2,1)} %param.11), kind=kOutput, calls=%fused_computation.21 | convolution fusion | flops 1073872896 | bytes 6553600 | tf_op jit(solution)/shard_map/dot_general | solution.py:108
  77.9 1.8 copy.50
  79.7 2.0 %fusion.16 = f32[768,1,128]{0,2,1:T(8,128)S(1)} fusion(bf16[256,4,128]{0,2,1:T(8,128)(2,1)} %bitcast.143, f32[4,256]{1,0:T(4,128)S(1)} %get-tuple-element.42, f32[768,256,4]{1,0,2:T(8,128)S(1)} %get-tuple-element.43, pred[256,768]{0,1:T(8,128)(4,1)} %copy-done.1), kind=kOutput, calls=%fused_computation.18 | convolution fusion | flops 204472320 | bytes 4001792 | tf_op jit(solution)/shard_map/kgst,skgd->tkd/dot_general | solution.py:85
  82.8 2.8 %fusion.7 = bf16[4,256,768]{1,2,0:T(8,128)(2,1)S(1)} fusion(f32[768,256,4]{1,0,2:T(8,128)S(1)} %get-tuple-element.45, f32[4,256]{1,0:T(4,128)S(1)} %get-tuple-element.44, f32[4,256]{1,0:T(4,128)S(1)} %get-tuple-element.42, f32[768,256,4]{1,0,2:T(8,128)} %copy-done, pred[256,768]{0,1:T(8,128)(4,1)S(1)} %copy-done.2), kind=kLoop, calls=%fused_computation.11 | loop fusion | flops 5505024 | bytes 8069120 | tf_op jit(solution)/shard_map/reshape.9
  86.4 3.4 %collective-permute-start.4 = (f32[128,256]{0,1:T(8,128)S(1)}, f32[128,256]{0,1:T(8,128)S(1)}, u32[]{:S(2)}, u32[]{:S(2)}) collective-permute-start(f32[128,256]{0,1:T(8,128)S(1)} %pad_maximum_fusion), channel_id=1, source_target_pairs={{1,0},{2,1},{3,2},{4,3},{5,4},{6,5},{7,6},{64,7},{65,64},{66,65},{... | collective-permute-start | bytes 393224 | tf_op jit(solution)/shard_map/ppermute | solution.py:16
  89.7 4.2 %collective-permute-start.5 = (f32[128,256]{0,1:T(8,128)S(1)}, f32[128,256]{0,1:T(8,128)S(1)}, u32[]{:S(2)}, u32[]{:S(2)}) collective-permute-start(f32[128,256]{0,1:T(8,128)S(1)} %pad_maximum_fusion.1), channel_id=1, source_target_pairs={{2,0},{3,1},{4,2},{5,3},{6,4},{7,5},{64,6},{65,7},{66,64},{67,65},... | collective-permute-start | bytes 393224 | tf_op jit(solution)/shard_map/ppermute | solution.py:16
  94.0 2.6 %collective-permute-start.6 = (f32[128,256]{0,1:T(8,128)S(1)}, f32[128,256]{0,1:T(8,128)S(1)}, u32[]{:S(2)}, u32[]{:S(2)}) collective-permute-start(f32[128,256]{0,1:T(8,128)S(1)} %pad_maximum_fusion.2), channel_id=1, source_target_pairs={{3,0},{4,1},{5,2},{6,3},{7,4},{64,5},{65,6},{66,7},{67,64},{68,65}... | collective-permute-start | bytes 393224 | tf_op jit(solution)/shard_map/ppermute | solution.py:16
  96.7 1.9 %collective-permute-start.7 = (f32[128,256]{0,1:T(8,128)S(1)}, f32[128,256]{0,1:T(8,128)S(1)}, u32[]{:S(2)}, u32[]{:S(2)}) collective-permute-start(f32[128,256]{0,1:T(8,128)S(1)} %pad_maximum_fusion.3), channel_id=1, source_target_pairs={{4,0},{5,1},{6,2},{7,3},{64,4},{65,5},{66,6},{67,7},{68,64},{69,65... | collective-permute-start | bytes 393224 | tf_op jit(solution)/shard_map/ppermute | solution.py:16
  99.8 6.2 %collective-permute-done.6 = f32[128,256]{0,1:T(8,128)S(1)} collective-permute-done((f32[128,256]{0,1:T(8,128)S(1)}, f32[128,256]{0,1:T(8,128)S(1)}, u32[]{:S(2)}, u32[]{:S(2)}) %collective-permute-start.6) | collective-permute-done | bytes 131104 | tf_op jit(solution)/shard_map/ppermute | solution.py:16
  106.0 4.7 %collective-permute-done.7 = f32[128,256]{0,1:T(8,128)S(1)} collective-permute-done((f32[128,256]{0,1:T(8,128)S(1)}, f32[128,256]{0,1:T(8,128)S(1)}, u32[]{:S(2)}, u32[]{:S(2)}) %collective-permute-start.7) | collective-permute-done | bytes 131104 | tf_op jit(solution)/shard_map/ppermute | solution.py:16
  110.7 32.7 %reduce-scatter.2.cloned.1.call-done = bf16[256,512]{0,1:T(8,128)(2,1)} async-done(((bf16[4096,512]{0,1:T(8,128)(2,1)}), bf16[256,512]{0,1:T(8,128)(2,1)}) %reduce-scatter.2.cloned.1.call-update) | async-done | bytes 262160 | tf_op jit(solution)/shard_map/reduce_scatter | solution.py:135
  144.5 3.2 %collective-permute-start.8 = (f32[256,256]{1,0:T(8,128)S(1)}, f32[256,256]{1,0:T(8,128)S(1)}, u32[]{:S(2)}, u32[]{:S(2)}) collective-permute-start(f32[256,256]{1,0:T(8,128)S(1)} %bitcast.142), channel_id=1, source_target_pairs={{0,1},{1,0},{2,3},{3,2},{4,5},{5,4},{6,7},{7,6},{8,9},{9,8},{10,11... | collective-permute-start | bytes 786440 | tf_op jit(solution)/shard_map/ppermute | solution.py:33
  147.7 5.0 %collective-permute-done.8 = f32[256,256]{1,0:T(8,128)S(1)} collective-permute-done((f32[256,256]{1,0:T(8,128)S(1)}, f32[256,256]{1,0:T(8,128)S(1)}, u32[]{:S(2)}, u32[]{:S(2)}) %collective-permute-start.8) | collective-permute-done | bytes 262176 | tf_op jit(solution)/shard_map/ppermute | solution.py:33
  152.8 4.2 %collective-permute-start.9 = (f32[128,256]{1,0:T(8,128)S(1)}, f32[128,256]{1,0:T(8,128)S(1)}, u32[]{:S(2)}, u32[]{:S(2)}) collective-permute-start(f32[128,256]{1,0:T(8,128)S(1)} %slice_select_fusion.2), channel_id=1, source_target_pairs={{0,2},{1,3},{2,0},{3,1},{4,6},{5,7},{6,4},{7,5},{8,10},{9,11},{10,... | collective-permute-start | bytes 393224 | tf_op jit(solution)/shard_map/ppermute | solution.py:33
  157.1 5.0 %collective-permute-done.9 = f32[128,256]{1,0:T(8,128)S(1)} collective-permute-done((f32[128,256]{1,0:T(8,128)S(1)}, f32[128,256]{1,0:T(8,128)S(1)}, u32[]{:S(2)}, u32[]{:S(2)}) %collective-permute-start.9) | collective-permute-done | bytes 131104 | tf_op jit(solution)/shard_map/ppermute | solution.py:33
  162.1 4.8 %collective-permute-start.10 = (f32[64,256]{1,0:T(8,128)S(1)}, f32[64,256]{1,0:T(8,128)S(1)}, u32[]{:S(2)}, u32[]{:S(2)}) collective-permute-start(f32[64,256]{1,0:T(8,128)S(1)} %slice_select_fusion.3), channel_id=1, source_target_pairs={{0,4},{1,5},{2,6},{3,7},{4,0},{5,1},{6,2},{7,3},{8,12},{9,13},{10,... | collective-permute-start | bytes 196616 | tf_op jit(solution)/shard_map/ppermute | solution.py:33
  169.7 2.7 %collective-permute-done.10 = f32[64,256]{1,0:T(8,128)S(1)} collective-permute-done((f32[64,256]{1,0:T(8,128)S(1)}, f32[64,256]{1,0:T(8,128)S(1)}, u32[]{:S(2)}, u32[]{:S(2)}) %collective-permute-start.10) | collective-permute-done | bytes 65568 | tf_op jit(solution)/shard_map/ppermute | solution.py:33
  (71 shorter events, 15.2 us)
Async XLA Ops:
  7.2 61.0 %all-gather.2.cloned.1.call-start = ((), (), s32[]{:S(2)}) async-start(), calls=%async_computation.1 | async-start | bytes 2359296 | tf_op jit(solution)/shard_map/all_gather | solution.py:107
  7.9 135.5 %reduce-scatter.2.cloned.1.call-start = ((), (), s32[]{:S(2)}) async-start(), calls=%async_computation.2 | async-start | bytes 4456448 | tf_op jit(solution)/shard_map/reduce_scatter | solution.py:135
  9.5 20.8 %collective-permute-start = (bf16[128,256]{1,0:T(8,128)(2,1)S(1)}, bf16[128,256]{1,0:T(8,128)(2,1)S(1)}, u32[]{:S(2)}, u32[]{:S(2)}) collective-permute-start(bf16[128,256]{1,0:T(8,128)(2,1)S(1)} %pad_maximum_fusion.4), channel_id=1, source_target_pairs={{0,1},{1,2},{2,3},{3,4},{4,5},{5,6},{6,7},{7,64},{64,65},{65,66},{... | collective-permute-start | bytes 196616 | tf_op jit(solution)/shard_map/ppermute | solution.py:16
  11.4 18.9 %collective-permute-start.1 = (bf16[128,256]{1,0:T(8,128)(2,1)S(1)}, bf16[128,256]{1,0:T(8,128)(2,1)S(1)}, u32[]{:S(2)}, u32[]{:S(2)}) collective-permute-start(bf16[128,256]{1,0:T(8,128)(2,1)S(1)} %pad_maximum_fusion.4), channel_id=1, source_target_pairs={{0,2},{1,3},{2,4},{3,5},{4,6},{5,7},{6,64},{7,65},{64,66},{65,67},... | collective-permute-start | bytes 196616 | tf_op jit(solution)/shard_map/ppermute | solution.py:16
  15.3 15.0 %collective-permute-start.2 = (bf16[128,256]{1,0:T(8,128)(2,1)S(1)}, bf16[128,256]{1,0:T(8,128)(2,1)S(1)}, u32[]{:S(2)}, u32[]{:S(2)}) collective-permute-start(bf16[128,256]{1,0:T(8,128)(2,1)S(1)} %pad_maximum_fusion.4), channel_id=1, source_target_pairs={{0,3},{1,4},{2,5},{3,6},{4,7},{5,64},{6,65},{7,66},{64,67},{65,68}... | collective-permute-start | bytes 196616 | tf_op jit(solution)/shard_map/ppermute | solution.py:16
  20.5 10.6 %collective-permute-start.3 = (bf16[128,256]{1,0:T(8,128)(2,1)S(1)}, bf16[128,256]{1,0:T(8,128)(2,1)S(1)}, u32[]{:S(2)}, u32[]{:S(2)}) collective-permute-start(bf16[128,256]{1,0:T(8,128)(2,1)S(1)} %pad_maximum_fusion.4), channel_id=1, source_target_pairs={{0,4},{1,5},{2,6},{3,7},{4,64},{5,65},{6,66},{7,67},{64,68},{65,69... | collective-permute-start | bytes 196616 | tf_op jit(solution)/shard_map/ppermute | solution.py:16
  29.3 3.4 %copy-start.1 = (pred[256,768]{0,1:T(8,128)(4,1)}, pred[256,768]{0,1:T(8,128)(4,1)S(1)}, u32[]{:S(2)}) copy-start(pred[256,768]{0,1:T(8,128)(4,1)S(1)} %pad_add_fusion) | copy-start | bytes 589828
  31.1 0.7 copy-start.3
  31.2 1.5 copy-start.6
  32.6 49.2 %copy-start = (f32[768,256,4]{1,0,2:T(8,128)}, f32[768,256,4]{1,0,2:T(8,128)S(1)}, u32[]{:S(2)}) copy-start(f32[768,256,4]{1,0,2:T(8,128)S(1)} %get-tuple-element.43) | copy-start | bytes 9437188
  79.7 2.1 %copy-start.2 = (pred[256,768]{0,1:T(8,128)(4,1)S(1)}, pred[256,768]{0,1:T(8,128)(4,1)}, u32[]{:S(2)}) copy-start(pred[256,768]{0,1:T(8,128)(4,1)} %copy-done.1) | copy-start | bytes 589828
  79.7 2.1 %copy-start.5 = (bf16[256,512]{0,1:T(8,128)(2,1)S(1)}, bf16[256,512]{0,1:T(8,128)(2,1)}, u32[]{:S(2)}) copy-start(bf16[256,512]{0,1:T(8,128)(2,1)} %copy.50) | copy-start | bytes 786436
  79.7 2.1 %copy-start.7 = (bf16[768,128]{1,0:T(8,128)(2,1)S(1)}, bf16[768,128]{1,0:T(8,128)(2,1)}, u32[]{:S(2)}) copy-start(bf16[768,128]{1,0:T(8,128)(2,1)} %copy-done.6) | copy-start | bytes 589828
  86.4 12.3 %collective-permute-start.4 = (f32[128,256]{0,1:T(8,128)S(1)}, f32[128,256]{0,1:T(8,128)S(1)}, u32[]{:S(2)}, u32[]{:S(2)}) collective-permute-start(f32[128,256]{0,1:T(8,128)S(1)} %pad_maximum_fusion), channel_id=1, source_target_pairs={{1,0},{2,1},{3,2},{4,3},{5,4},{6,5},{7,6},{64,7},{65,64},{66,65},{... | collective-permute-start | bytes 393224 | tf_op jit(solution)/shard_map/ppermute | solution.py:16
  89.7 10.0 %collective-permute-start.5 = (f32[128,256]{0,1:T(8,128)S(1)}, f32[128,256]{0,1:T(8,128)S(1)}, u32[]{:S(2)}, u32[]{:S(2)}) collective-permute-start(f32[128,256]{0,1:T(8,128)S(1)} %pad_maximum_fusion.1), channel_id=1, source_target_pairs={{2,0},{3,1},{4,2},{5,3},{6,4},{7,5},{64,6},{65,7},{66,64},{67,65},... | collective-permute-start | bytes 393224 | tf_op jit(solution)/shard_map/ppermute | solution.py:16
  94.0 73.0 %copy-start.4 = (bf16[768,128]{1,0:T(8,128)(2,1)S(1)}, bf16[768,128]{1,0:T(8,128)(2,1)}, u32[]{:S(2)}) copy-start(bf16[768,128]{1,0:T(8,128)(2,1)} %copy-done.3) | copy-start | bytes 589828
  94.0 12.0 %collective-permute-start.6 = (f32[128,256]{0,1:T(8,128)S(1)}, f32[128,256]{0,1:T(8,128)S(1)}, u32[]{:S(2)}, u32[]{:S(2)}) collective-permute-start(f32[128,256]{0,1:T(8,128)S(1)} %pad_maximum_fusion.2), channel_id=1, source_target_pairs={{3,0},{4,1},{5,2},{6,3},{7,4},{64,5},{65,6},{66,7},{67,64},{68,65}... | collective-permute-start | bytes 393224 | tf_op jit(solution)/shard_map/ppermute | solution.py:16
  96.7 14.0 %collective-permute-start.7 = (f32[128,256]{0,1:T(8,128)S(1)}, f32[128,256]{0,1:T(8,128)S(1)}, u32[]{:S(2)}, u32[]{:S(2)}) collective-permute-start(f32[128,256]{0,1:T(8,128)S(1)} %pad_maximum_fusion.3), channel_id=1, source_target_pairs={{4,0},{5,1},{6,2},{7,3},{64,4},{65,5},{66,6},{67,7},{68,64},{69,65... | collective-permute-start | bytes 393224 | tf_op jit(solution)/shard_map/ppermute | solution.py:16
  144.5 8.3 %collective-permute-start.8 = (f32[256,256]{1,0:T(8,128)S(1)}, f32[256,256]{1,0:T(8,128)S(1)}, u32[]{:S(2)}, u32[]{:S(2)}) collective-permute-start(f32[256,256]{1,0:T(8,128)S(1)} %bitcast.142), channel_id=1, source_target_pairs={{0,1},{1,0},{2,3},{3,2},{4,5},{5,4},{6,7},{7,6},{8,9},{9,8},{10,11... | collective-permute-start | bytes 786440 | tf_op jit(solution)/shard_map/ppermute | solution.py:33
  152.8 9.3 %collective-permute-start.9 = (f32[128,256]{1,0:T(8,128)S(1)}, f32[128,256]{1,0:T(8,128)S(1)}, u32[]{:S(2)}, u32[]{:S(2)}) collective-permute-start(f32[128,256]{1,0:T(8,128)S(1)} %slice_select_fusion.2), channel_id=1, source_target_pairs={{0,2},{1,3},{2,0},{3,1},{4,6},{5,7},{6,4},{7,5},{8,10},{9,11},{10,... | collective-permute-start | bytes 393224 | tf_op jit(solution)/shard_map/ppermute | solution.py:33
  162.1 10.3 %collective-permute-start.10 = (f32[64,256]{1,0:T(8,128)S(1)}, f32[64,256]{1,0:T(8,128)S(1)}, u32[]{:S(2)}, u32[]{:S(2)}) collective-permute-start(f32[64,256]{1,0:T(8,128)S(1)} %slice_select_fusion.3), channel_id=1, source_target_pairs={{0,4},{1,5},{2,6},{3,7},{4,0},{5,1},{6,2},{7,3},{8,12},{9,13},{10,... | collective-permute-start | bytes 196616 | tf_op jit(solution)/shard_map/ppermute | solution.py:33
Sparse Core Ops, SparseCore 0:
  10.7 57.4 all-gather.1
  73.2 70.1 reduce-scatter.1
